TPU v7x, 512 devices: a whole 4x4x16 slice. The times are simulated.
512 devices in a mesh: row: 32 (over z_lo, y), col: 16 (over z_hi, x, core).
Axes of the slice: x: 4, y: 4, z: 16 (z_hi: 2, z_lo: 8; z = z_hi * 8 + z_lo), core: 2. Of those that a mesh axis runs over, the one named last changes fastest.
Arguments:
- rhs: bfloat16 [32, 16, 64, 768], P('row', 'col'), may hold values from -6 to 6
- operator_blocks: bfloat16 [32, 16, 768, 768], P('row', 'col'), may hold values from -0.5 to 3.5
- local_solver: bfloat16 [32, 16, 768, 768], P('row', 'col'), may hold values from -0.1 to 0.6
- modes: bfloat16 [32, 16, 48, 768], P('row', 'col'), may hold values from -0.21875 to 0.21875
- coupling: bfloat16 [32, 16, 4, 128, 128], P('row', 'col'), may hold values from -0.25 to 0.25
- coarse_inverse: bfloat16 [16, 1536, 32, 768], P('col', None, 'row'), may hold values from -0.05 to 0.15
- send_block: int32 [32, 16, 8], P('row', 'col'), may hold values from 0 to 5
- slot_dir: int32 [32, 16, 4], P('row', 'col'), may hold values from -1 to 7, as said below
- slot_block: int32 [32, 16, 4], P('row', 'col'), may hold values from 0 to 5
Outputs:
- solution: float32 [32, 16, 64, 768], P('row', 'col')
Inputs may be any that keep to these rules, and one draw needn't show every extreme that they name: `slot_dir`: each subdomain lists 2 to 4 distinct directions toward subdomains inside the grid in its first slots; the remaining slots hold -1.
All inputs are finite; a program needn't handle non-finite values.
Results may differ from a plain program's by a relative error of at most 0.0033.
Values may be sent and summed in bfloat16 or wider, within the bound.
No kernel may reach another device: no remote copies, remote signals or barrier semaphores. Data moves between devices by JAX's collectives and lax.ppermute only.
A program may use at most 64 MiB of HBM per device.

v0:
```python
import jax
import jax.numpy as jnp
from jax import lax
from jax.sharding import PartitionSpec as P

ITERS = 6
OFFSETS = ((-1, -1), (-1, 0), (-1, 1), (0, -1), (0, 1), (1, -1), (1, 0), (1, 1))


def passed_along(block, axis, distance):
    devices = range(lax.axis_size(axis))
    route = [(i - distance, i) for i in devices if i - distance in devices]
    return lax.ppermute(block, axis, route)


def hop_rows(portion, steps):
    return passed_along(portion, "row", steps)


def hop_cols(portion, steps):
    return passed_along(portion, "col", steps)


def neighbour_pieces(outgoing):
    arrived = []
    for direction in range(8):
        shift_a, shift_b = OFFSETS[direction]
        portion = outgoing[7 - direction]
        if shift_a != 0:
            portion = hop_rows(portion, -shift_a)
        if shift_b != 0:
            portion = hop_cols(portion, -shift_b)
        arrived.append(portion)
    return jnp.stack(arrived, 0)


def on_device(
    rhs,
    operator_blocks,
    local_solver,
    modes,
    coupling,
    coarse_inverse,
    send_block,
    slot_dir,
    slot_block,
):
    highest = lax.Precision.HIGHEST
    columns = rhs.shape[2]
    unknowns = rhs.shape[3]
    block_size = coupling.shape[3]
    block_count = unknowns // block_size
    mode_count = modes.shape[2]
    piece_rows = mode_count * columns // 128
    rhs_full = rhs[0, 0].astype(jnp.float32)
    operator_matrix = operator_blocks[0, 0]
    solver_matrix = local_solver[0, 0]
    mode_basis = modes[0, 0]
    couplings = coupling[0, 0]
    coarse_tile = coarse_inverse[0, :, 0, :]
    send_onehot = (send_block[0, 0][:, None] == jnp.arange(block_count)[None, :]).astype(
        jnp.bfloat16
    )
    dir_onehot = (slot_dir[0, 0][:, None] == jnp.arange(8)[None, :]).astype(jnp.bfloat16)
    block_onehot = (slot_block[0, 0][:, None] == jnp.arange(block_count)[None, :]).astype(
        jnp.float32
    )
    col_index = lax.axis_index("col")

    def coarse_solve(rounded):
        restricted = lax.dot_general(
            mode_basis, rounded, (((1,), (1,)), ((), ())), preferred_element_type=jnp.float32
        )
        flat_piece = restricted.astype(jnp.bfloat16).reshape(piece_rows, 128)
        gathered = lax.all_gather(flat_piece, "row", axis=0, tiled=True).reshape(-1, columns)
        partial_sums = lax.dot_general(
            coarse_tile, gathered, (((0,), (0,)), ((), ())), preferred_element_type=jnp.float32
        )
        summed = lax.psum(partial_sums.reshape(-1, 128), "col")
        own_rows = lax.dynamic_slice_in_dim(summed, col_index * piece_rows, piece_rows, 0)
        return own_rows.reshape(mode_count, columns).astype(jnp.bfloat16)

    solution = jnp.zeros((columns, unknowns), jnp.float32)
    pending = None
    for iteration in range(ITERS):
        if iteration == 0:
            residual = rhs_full
        else:
            field_half = solution.astype(jnp.bfloat16)
            blocks = field_half.reshape(columns, block_count, block_size)
            outgoing = jnp.einsum(
                "ckn,ek->ecn", blocks, send_onehot, preferred_element_type=jnp.float32
            ).astype(jnp.bfloat16)
            incoming = neighbour_pieces(outgoing)
            chosen = jnp.einsum(
                "sd,dcn->scn", dir_onehot, incoming, preferred_element_type=jnp.float32
            ).astype(jnp.bfloat16)
            coupled = jnp.einsum(
                "scn,snm->scm", chosen, couplings, preferred_element_type=jnp.float32
            )
            placed = jnp.einsum("scm,sk->ckm", coupled, block_onehot, precision=highest).reshape(
                columns, unknowns
            )
            residual = rhs_full - (
                jnp.dot(field_half, operator_matrix, preferred_element_type=jnp.float32) + placed
            )
        rounded = residual.astype(jnp.bfloat16)
        update = jnp.dot(rounded, solver_matrix, preferred_element_type=jnp.float32)
        fresh = coarse_solve(rounded) if iteration + 1 < ITERS else None
        if pending is not None:
            update = update + lax.dot_general(
                pending, mode_basis, (((0,), (0,)), ((), ())), preferred_element_type=jnp.float32
            )
        solution = solution + update
        pending = fresh
    return solution[None, None]


def solution(mesh):
    in_specs = (
        P("row", "col", None, None),
        P("row", "col", None, None),
        P("row", "col", None, None),
        P("row", "col", None, None),
        P("row", "col", None, None, None),
        P("col", None, "row", None),
        P("row", "col", None),
        P("row", "col", None),
        P("row", "col", None),
    )
    out_specs = P("row", "col", None, None)
    return jax.shard_map(
        on_device, mesh=mesh, in_specs=in_specs, out_specs=out_specs, check_vma=False
    )
```

profile of v0, /device:TPU:23, one launch (start us, length us, event | category | flops | bytes accessed | tf_op | source)
XLA Modules:
  0.0 1464.4 jit_solution(8940192979941187941)
XLA Ops:
  0.0 2.5 fusion.173
  3.6 2.9 collective-permute-start
  6.5 3.2 collective-permute-start.3
  9.8 2.1 collective-permute-start.7
  11.9 2.4 collective-permute-start.10
  14.3 2.9 collective-permute-start.2
  17.5 100.3 %all_gather.15 = bf16[768,128]{1,0:T(8,128)(2,1)S(1)} all-gather(bf16[24,128]{1,0:T(8,128)(2,1)S(1)} %reshape.90), channel_id=1, replica_groups=mesh['row'=32,'col'=16] {'row'}, dimensions={0}, use_global_device_ids=true | all-gather | bytes 202752 | tf_op jit(solution)/shard_map/all_gather | solution.py:75
  118.7 23.7 %collective-permute-start.5 = (bf16[64,128]{1,0:T(8,128)(2,1)S(1)}, bf16[64,128]{1,0:T(8,128)(2,1)S(1)}, u32[]{:S(2)}, u32[]{:S(2)}) collective-permute-start(bf16[64,128]{1,0:T(8,128)(2,1)S(1)} %bitcast.406), channel_id=1, source_target_pairs={{0,1},{1,2},{2,3},{3,4},{4,5},{5,6},{6,7},{7,8},{8,9},{9,10},{10,1... | collective-permute-start | bytes 49160 | tf_op jit(solution)/shard_map/ppermute | solution.py:13
  144.4 124.1 %all-reduce.5 = bf16[384,128]{1,0:T(8,128)(2,1)S(1)} all-reduce(f32[384,128]{1,0:T(8,128)S(1)} %reshape.92), channel_id=1, replica_groups=mesh['row'=32,'col'=16] {'col'}, use_global_device_ids=true, to_apply=%region_0.0 | all-reduce | flops 49152 | bytes 294912 | tf_op jit(solution)/shard_map/psum | solution.py:79
  268.5 8.2 collective-permute-start.9
  276.8 14.8 %collective-permute-start.1 = (bf16[64,128]{1,0:T(8,128)(2,1)S(1)}, bf16[64,128]{1,0:T(8,128)(2,1)S(1)}, u32[]{:S(2)}, u32[]{:S(2)}) collective-permute-start(bf16[64,128]{1,0:T(8,128)(2,1)S(1)} %collective-permute-done), channel_id=1, source_target_pairs={{0,1},{1,2},{2,3},{3,4},{4,5},{5,6},{6,7},{7,8},{8,9},{9,10},{10,1... | collective-permute-start | bytes 49160 | tf_op jit(solution)/shard_map/ppermute | solution.py:13
  293.5 14.5 collective-permute-start.8
  310.3 13.6 collective-permute-done.11
  340.2 5.8 collective-permute-start.19
  346.5 3.9 collective-permute-start.22
  354.9 2.8 collective-permute-start.17
  357.7 1.9 collective-permute-start.18
  359.6 96.8 %all_gather.16 = bf16[768,128]{1,0:T(8,128)(2,1)} all-gather(bf16[24,128]{1,0:T(8,128)(2,1)} %reshape.95), channel_id=1, replica_groups=mesh['row'=32,'col'=16] {'row'}, dimensions={0}, use_global_device_ids=true | all-gather | bytes 202752 | tf_op jit(solution)/shard_map/all_gather | solution.py:75
  459.7 10.7 collective-permute-start.21
  470.4 28.7 %collective-permute-start.13 = (bf16[64,128]{1,0:T(8,128)(2,1)}, bf16[64,128]{1,0:T(8,128)(2,1)}, u32[]{:S(2)}, u32[]{:S(2)}) collective-permute-start(bf16[64,128]{1,0:T(8,128)(2,1)} %collective-permute-done.12), channel_id=1, source_target_pairs={{0,1},{1,2},{2,3},{3,4},{4,5},{5,6},{6,7},{7,8},{8,9},{9,10},{10,1... | collective-permute-start | bytes 49160 | tf_op jit(solution)/shard_map/ppermute | solution.py:13
  499.1 1.9 collective-permute-start.16
  501.1 14.5 collective-permute-start.20
  515.5 1.9 collective-permute-start.23
  517.5 2.2 fusion.35
  541.5 95.9 %all_gather.17 = bf16[768,128]{1,0:T(8,128)(2,1)} all-gather(bf16[24,128]{1,0:T(8,128)(2,1)} %reshape.100), channel_id=1, replica_groups=mesh['row'=32,'col'=16] {'row'}, dimensions={0}, use_global_device_ids=true | all-gather | bytes 202752 | tf_op jit(solution)/shard_map/all_gather | solution.py:75
  639.3 2.1 fusion.38
  645.1 141.5 %all-reduce.6 = (bf16[384,128]{1,0:T(8,128)(2,1)}, bf16[384,128]{1,0:T(8,128)(2,1)}) all-reduce(f32[384,128]{1,0:T(8,128)} %reshape.97, f32[384,128]{1,0:T(8,128)} %reshape.102), channel_id=1, replica_groups=mesh['row'=32,'col'=16] {'col'}, use_global_device_ids=true, to_apply=%region_1.0 | all-reduce | flops 98304 | bytes 589824 | tf_op jit(solution)/shard_map/psum | solution.py:79
  788.7 2.0 fusion.175
  793.7 1.9 collective-permute-start.24
  795.7 1.9 collective-permute-start.27
  797.6 9.7 collective-permute-start.31
  807.4 4.2 collective-permute-start.34
  813.5 15.0 %collective-permute-start.29 = (bf16[64,128]{1,0:T(8,128)(2,1)S(1)}, bf16[64,128]{1,0:T(8,128)(2,1)S(1)}, u32[]{:S(2)}, u32[]{:S(2)}) collective-permute-start(bf16[64,128]{1,0:T(8,128)(2,1)S(1)} %bitcast.427), channel_id=1, source_target_pairs={{0,1},{1,2},{2,3},{3,4},{4,5},{5,6},{6,7},{7,8},{8,9},{9,10},{10,1... | collective-permute-start | bytes 49160 | tf_op jit(solution)/shard_map/ppermute | solution.py:13
  831.1 3.6 collective-permute-start.33
  834.8 14.7 %collective-permute-start.25 = (bf16[64,128]{1,0:T(8,128)(2,1)}, bf16[64,128]{1,0:T(8,128)(2,1)}, u32[]{:S(2)}, u32[]{:S(2)}) collective-permute-start(bf16[64,128]{1,0:T(8,128)(2,1)} %collective-permute-done.24), channel_id=1, source_target_pairs={{0,1},{1,2},{2,3},{3,4},{4,5},{5,6},{6,7},{7,8},{8,9},{9,10},{10,1... | collective-permute-start | bytes 49160 | tf_op jit(solution)/shard_map/ppermute | solution.py:13
  849.5 1.9 collective-permute-start.28
  851.5 14.5 collective-permute-start.32
  866.0 2.1 collective-permute-start.35
  879.7 2.5 collective-permute-done.35
  898.4 2.9 collective-permute-start.39
  903.0 2.4 collective-permute-start.43
  906.0 3.9 collective-permute-start.46
  914.4 13.1 collective-permute-start.41
  927.5 1.9 collective-permute-start.42
  929.4 97.0 %all_gather.18 = bf16[768,128]{1,0:T(8,128)(2,1)} all-gather(bf16[24,128]{1,0:T(8,128)(2,1)} %reshape.105), channel_id=1, replica_groups=mesh['row'=32,'col'=16] {'row'}, dimensions={0}, use_global_device_ids=true | all-gather | bytes 202752 | tf_op jit(solution)/shard_map/all_gather | solution.py:75
  1029.7 10.7 collective-permute-start.45
  1040.5 28.5 %collective-permute-start.37 = (bf16[64,128]{1,0:T(8,128)(2,1)}, bf16[64,128]{1,0:T(8,128)(2,1)}, u32[]{:S(2)}, u32[]{:S(2)}) collective-permute-start(bf16[64,128]{1,0:T(8,128)(2,1)} %collective-permute-done.36), channel_id=1, source_target_pairs={{0,1},{1,2},{2,3},{3,4},{4,5},{5,6},{6,7},{7,8},{8,9},{9,10},{10,1... | collective-permute-start | bytes 49160 | tf_op jit(solution)/shard_map/ppermute | solution.py:13
  1068.9 1.9 collective-permute-start.40
  1070.9 14.5 collective-permute-start.44
  1085.4 1.9 collective-permute-start.47
  1087.3 2.2 fusion.41
  1111.3 96.5 %all_gather.19 = bf16[768,128]{1,0:T(8,128)(2,1)} all-gather(bf16[24,128]{1,0:T(8,128)(2,1)} %reshape.110), channel_id=1, replica_groups=mesh['row'=32,'col'=16] {'row'}, dimensions={0}, use_global_device_ids=true | all-gather | bytes 202752 | tf_op jit(solution)/shard_map/all_gather | solution.py:75
  1209.7 2.1 fusion.44
  1215.5 141.9 %all-reduce.7 = (bf16[384,128]{1,0:T(8,128)(2,1)}, bf16[384,128]{1,0:T(8,128)(2,1)}) all-reduce(f32[384,128]{1,0:T(8,128)} %reshape.107, f32[384,128]{1,0:T(8,128)} %reshape.112), channel_id=1, replica_groups=mesh['row'=32,'col'=16] {'col'}, use_global_device_ids=true, to_apply=%region_3.0 | all-reduce | flops 98304 | bytes 589824 | tf_op jit(solution)/shard_map/psum | solution.py:79
  1359.5 2.0 fusion.177
  1368.4 9.5 collective-permute-start.55
  1377.9 4.7 collective-permute-start.58
  1384.5 15.0 %collective-permute-start.53 = (bf16[64,128]{1,0:T(8,128)(2,1)S(1)}, bf16[64,128]{1,0:T(8,128)(2,1)S(1)}, u32[]{:S(2)}, u32[]{:S(2)}) collective-permute-start(bf16[64,128]{1,0:T(8,128)(2,1)S(1)} %bitcast.428), channel_id=1, source_target_pairs={{0,1},{1,2},{2,3},{3,4},{4,5},{5,6},{6,7},{7,8},{8,9},{9,10},{10,1... | collective-permute-start | bytes 49160 | tf_op jit(solution)/shard_map/ppermute | solution.py:13
  1402.1 3.6 collective-permute-start.57
  1405.8 14.7 %collective-permute-start.49 = (bf16[64,128]{1,0:T(8,128)(2,1)}, bf16[64,128]{1,0:T(8,128)(2,1)}, u32[]{:S(2)}, u32[]{:S(2)}) collective-permute-start(bf16[64,128]{1,0:T(8,128)(2,1)} %collective-permute-done.48), channel_id=1, source_target_pairs={{0,1},{1,2},{2,3},{3,4},{4,5},{5,6},{6,7},{7,8},{8,9},{9,10},{10,1... | collective-permute-start | bytes 49160 | tf_op jit(solution)/shard_map/ppermute | solution.py:13
  1422.5 14.5 collective-permute-start.56
  1449.2 4.0 collective-permute-done.59
  1459.8 2.6 fusion.20
  1462.4 1.9 fusion.48
  (285 shorter events, 168.8 us)
Async XLA Ops:
  0.0 117.9 %copy-start = (bf16[1,1536,1,768]{3,1,2,0:T(8,128)(2,1)S(1)}, bf16[1,1536,1,768]{3,1,2,0:T(8,128)(2,1)}, u32[]{:S(2)}) copy-start(bf16[1,1536,1,768]{3,1,2,0:T(8,128)(2,1)} %param.14) | copy-start | bytes 7077892
  3.6 115.1 %collective-permute-start = (bf16[64,128]{1,0:T(8,128)(2,1)S(1)}, bf16[64,128]{1,0:T(8,128)(2,1)S(1)}, u32[]{:S(2)}, u32[]{:S(2)}) collective-permute-start(bf16[64,128]{1,0:T(8,128)(2,1)S(1)} %bitcast.426), channel_id=1, source_target_pairs={{0,16},{16,32},{32,48},{48,64},{64,80},{80,96},{96,112},{112,128},... | collective-permute-start | bytes 49160 | tf_op jit(solution)/shard_map/ppermute | solution.py:13
  6.5 135.9 %collective-permute-start.3 = (bf16[64,128]{1,0:T(8,128)(2,1)S(1)}, bf16[64,128]{1,0:T(8,128)(2,1)S(1)}, u32[]{:S(2)}, u32[]{:S(2)}) collective-permute-start(bf16[64,128]{1,0:T(8,128)(2,1)S(1)} %bitcast.424), channel_id=1, source_target_pairs={{0,16},{16,32},{32,48},{48,64},{64,80},{80,96},{96,112},{112,128},... | collective-permute-start | bytes 49160 | tf_op jit(solution)/shard_map/ppermute | solution.py:13
  9.8 258.8 %collective-permute-start.7 = (bf16[64,128]{1,0:T(8,128)(2,1)S(1)}, bf16[64,128]{1,0:T(8,128)(2,1)S(1)}, u32[]{:S(2)}, u32[]{:S(2)}) collective-permute-start(bf16[64,128]{1,0:T(8,128)(2,1)S(1)} %bitcast.404), channel_id=1, source_target_pairs={{16,0},{32,16},{48,32},{64,48},{80,64},{96,80},{112,96},{128,112},... | collective-permute-start | bytes 49160 | tf_op jit(solution)/shard_map/ppermute | solution.py:13
  11.9 264.9 %collective-permute-start.10 = (bf16[64,128]{1,0:T(8,128)(2,1)S(1)}, bf16[64,128]{1,0:T(8,128)(2,1)S(1)}, u32[]{:S(2)}, u32[]{:S(2)}) collective-permute-start(bf16[64,128]{1,0:T(8,128)(2,1)S(1)} %bitcast.403), channel_id=1, source_target_pairs={{16,0},{32,16},{48,32},{64,48},{80,64},{96,80},{112,96},{128,112},... | collective-permute-start | bytes 49160 | tf_op jit(solution)/shard_map/ppermute | solution.py:13
  14.3 277.3 %collective-permute-start.2 = (bf16[64,128]{1,0:T(8,128)(2,1)S(1)}, bf16[64,128]{1,0:T(8,128)(2,1)S(1)}, u32[]{:S(2)}, u32[]{:S(2)}) collective-permute-start(bf16[64,128]{1,0:T(8,128)(2,1)S(1)} %bitcast.401), channel_id=1, source_target_pairs={{0,16},{16,32},{32,48},{48,64},{64,80},{80,96},{96,112},{112,128},... | collective-permute-start | bytes 49160 | tf_op jit(solution)/shard_map/ppermute | solution.py:13
  118.4 205.9 %copy-start.22 = (s32[1,1,4]{2,1,0:T(1,128)S(1)}, s32[1,1,4]{2,1,0:T(1,128)}, u32[]{:S(2)}) copy-start(s32[1,1,4]{2,1,0:T(1,128)} %param.16) | copy-start | bytes 52
  118.7 174.8 %collective-permute-start.5 = (bf16[64,128]{1,0:T(8,128)(2,1)S(1)}, bf16[64,128]{1,0:T(8,128)(2,1)S(1)}, u32[]{:S(2)}, u32[]{:S(2)}) collective-permute-start(bf16[64,128]{1,0:T(8,128)(2,1)S(1)} %bitcast.406), channel_id=1, source_target_pairs={{0,1},{1,2},{2,3},{3,4},{4,5},{5,6},{6,7},{7,8},{8,9},{9,10},{10,1... | collective-permute-start | bytes 49160 | tf_op jit(solution)/shard_map/ppermute | solution.py:13
  142.5 165.5 %collective-permute-start.6 = (bf16[64,128]{1,0:T(8,128)(2,1)S(1)}, bf16[64,128]{1,0:T(8,128)(2,1)S(1)}, u32[]{:S(2)}, u32[]{:S(2)}) collective-permute-start(bf16[64,128]{1,0:T(8,128)(2,1)S(1)} %bitcast.402), channel_id=1, source_target_pairs={{1,0},{2,1},{3,2},{4,3},{5,4},{6,5},{7,6},{8,7},{9,8},{10,9},{11,1... | collective-permute-start | bytes 49160 | tf_op jit(solution)/shard_map/ppermute | solution.py:13
  268.5 41.6 %collective-permute-start.9 = (bf16[64,128]{1,0:T(8,128)(2,1)S(1)}, bf16[64,128]{1,0:T(8,128)(2,1)S(1)}, u32[]{:S(2)}, u32[]{:S(2)}) collective-permute-start(bf16[64,128]{1,0:T(8,128)(2,1)S(1)} %bitcast.408), channel_id=1, source_target_pairs={{16,0},{32,16},{48,32},{64,48},{80,64},{96,80},{112,96},{128,112},... | collective-permute-start | bytes 49160 | tf_op jit(solution)/shard_map/ppermute | solution.py:13
  276.8 33.4 %collective-permute-start.1 = (bf16[64,128]{1,0:T(8,128)(2,1)S(1)}, bf16[64,128]{1,0:T(8,128)(2,1)S(1)}, u32[]{:S(2)}, u32[]{:S(2)}) collective-permute-start(bf16[64,128]{1,0:T(8,128)(2,1)S(1)} %collective-permute-done), channel_id=1, source_target_pairs={{0,1},{1,2},{2,3},{3,4},{4,5},{5,6},{6,7},{7,8},{8,9},{9,10},{10,1... | collective-permute-start | bytes 49160 | tf_op jit(solution)/shard_map/ppermute | solution.py:13
  291.6 18.6 %collective-permute-start.4 = (bf16[64,128]{1,0:T(8,128)(2,1)S(1)}, bf16[64,128]{1,0:T(8,128)(2,1)S(1)}, u32[]{:S(2)}, u32[]{:S(2)}) collective-permute-start(bf16[64,128]{1,0:T(8,128)(2,1)S(1)} %collective-permute-done.3), channel_id=1, source_target_pairs={{1,0},{2,1},{3,2},{4,3},{5,4},{6,5},{7,6},{8,7},{9,8},{10,9},{11,1... | collective-permute-start | bytes 49160 | tf_op jit(solution)/shard_map/ppermute | solution.py:13
  293.5 16.8 %collective-permute-start.8 = (bf16[64,128]{1,0:T(8,128)(2,1)S(1)}, bf16[64,128]{1,0:T(8,128)(2,1)S(1)}, u32[]{:S(2)}, u32[]{:S(2)}) collective-permute-start(bf16[64,128]{1,0:T(8,128)(2,1)S(1)} %collective-permute-done.7), channel_id=1, source_target_pairs={{0,1},{1,2},{2,3},{3,4},{4,5},{5,6},{6,7},{7,8},{8,9},{9,10},{10,1... | collective-permute-start | bytes 49160 | tf_op jit(solution)/shard_map/ppermute | solution.py:13
  308.0 15.9 %collective-permute-start.11 = (bf16[64,128]{1,0:T(8,128)(2,1)S(1)}, bf16[64,128]{1,0:T(8,128)(2,1)S(1)}, u32[]{:S(2)}, u32[]{:S(2)}) collective-permute-start(bf16[64,128]{1,0:T(8,128)(2,1)S(1)} %collective-permute-done.10), channel_id=1, source_target_pairs={{1,0},{2,1},{3,2},{4,3},{5,4},{6,5},{7,6},{8,7},{9,8},{10,9},{11,1... | collective-permute-start | bytes 49160 | tf_op jit(solution)/shard_map/ppermute | solution.py:13
  334.0 20.9 %collective-permute-start.12 = (bf16[64,128]{1,0:T(8,128)(2,1)}, bf16[64,128]{1,0:T(8,128)(2,1)}, u32[]{:S(2)}, u32[]{:S(2)}) collective-permute-start(bf16[64,128]{1,0:T(8,128)(2,1)} %bitcast.385), channel_id=1, source_target_pairs={{0,16},{16,32},{32,48},{48,64},{64,80},{80,96},{96,112},{112,128},... | collective-permute-start | bytes 49160 | tf_op jit(solution)/shard_map/ppermute | solution.py:13
  336.5 21.1 %collective-permute-start.15 = (bf16[64,128]{1,0:T(8,128)(2,1)}, bf16[64,128]{1,0:T(8,128)(2,1)}, u32[]{:S(2)}, u32[]{:S(2)}) collective-permute-start(bf16[64,128]{1,0:T(8,128)(2,1)} %bitcast.383), channel_id=1, source_target_pairs={{0,16},{16,32},{32,48},{48,64},{64,80},{80,96},{96,112},{112,128},... | collective-permute-start | bytes 49160 | tf_op jit(solution)/shard_map/ppermute | solution.py:13
  340.2 119.5 %collective-permute-start.19 = (bf16[64,128]{1,0:T(8,128)(2,1)}, bf16[64,128]{1,0:T(8,128)(2,1)}, u32[]{:S(2)}, u32[]{:S(2)}) collective-permute-start(bf16[64,128]{1,0:T(8,128)(2,1)} %bitcast.380), channel_id=1, source_target_pairs={{16,0},{32,16},{48,32},{64,48},{80,64},{96,80},{112,96},{128,112},... | collective-permute-start | bytes 49160 | tf_op jit(solution)/shard_map/ppermute | solution.py:13
  346.5 123.8 %collective-permute-start.22 = (bf16[64,128]{1,0:T(8,128)(2,1)}, bf16[64,128]{1,0:T(8,128)(2,1)}, u32[]{:S(2)}, u32[]{:S(2)}) collective-permute-start(bf16[64,128]{1,0:T(8,128)(2,1)} %bitcast.378), channel_id=1, source_target_pairs={{16,0},{32,16},{48,32},{64,48},{80,64},{96,80},{112,96},{128,112},... | collective-permute-start | bytes 49160 | tf_op jit(solution)/shard_map/ppermute | solution.py:13
  351.1 148.0 %collective-permute-start.14 = (bf16[64,128]{1,0:T(8,128)(2,1)}, bf16[64,128]{1,0:T(8,128)(2,1)}, u32[]{:S(2)}, u32[]{:S(2)}) collective-permute-start(bf16[64,128]{1,0:T(8,128)(2,1)} %bitcast.384), channel_id=1, source_target_pairs={{0,16},{16,32},{32,48},{48,64},{64,80},{80,96},{96,112},{112,128},... | collective-permute-start | bytes 49160 | tf_op jit(solution)/shard_map/ppermute | solution.py:13
  354.9 146.2 %collective-permute-start.17 = (bf16[64,128]{1,0:T(8,128)(2,1)}, bf16[64,128]{1,0:T(8,128)(2,1)S(1)}, u32[]{:S(2)}, u32[]{:S(2)}) collective-permute-start(bf16[64,128]{1,0:T(8,128)(2,1)} %bitcast.419), channel_id=1, source_target_pairs={{0,1},{1,2},{2,3},{3,4},{4,5},{5,6},{6,7},{7,8},{8,9},{9,10},{10,1... | collective-permute-start | bytes 49160 | tf_op jit(solution)/shard_map/ppermute | solution.py:13
  357.7 157.9 %collective-permute-start.18 = (bf16[64,128]{1,0:T(8,128)(2,1)}, bf16[64,128]{1,0:T(8,128)(2,1)}, u32[]{:S(2)}, u32[]{:S(2)}) collective-permute-start(bf16[64,128]{1,0:T(8,128)(2,1)} %bitcast.413), channel_id=1, source_target_pairs={{1,0},{2,1},{3,2},{4,3},{5,4},{6,5},{7,6},{8,7},{9,8},{10,9},{11,1... | collective-permute-start | bytes 49160 | tf_op jit(solution)/shard_map/ppermute | solution.py:13
  459.7 67.0 %collective-permute-start.21 = (bf16[64,128]{1,0:T(8,128)(2,1)}, bf16[64,128]{1,0:T(8,128)(2,1)}, u32[]{:S(2)}, u32[]{:S(2)}) collective-permute-start(bf16[64,128]{1,0:T(8,128)(2,1)} %bitcast.416), channel_id=1, source_target_pairs={{16,0},{32,16},{48,32},{64,48},{80,64},{96,80},{112,96},{128,112},... | collective-permute-start | bytes 49160 | tf_op jit(solution)/shard_map/ppermute | solution.py:13
  470.4 57.6 %collective-permute-start.13 = (bf16[64,128]{1,0:T(8,128)(2,1)}, bf16[64,128]{1,0:T(8,128)(2,1)}, u32[]{:S(2)}, u32[]{:S(2)}) collective-permute-start(bf16[64,128]{1,0:T(8,128)(2,1)} %collective-permute-done.12), channel_id=1, source_target_pairs={{0,1},{1,2},{2,3},{3,4},{4,5},{5,6},{6,7},{7,8},{8,9},{9,10},{10,1... | collective-permute-start | bytes 49160 | tf_op jit(solution)/shard_map/ppermute | solution.py:13
  499.1 30.2 %collective-permute-start.16 = (bf16[64,128]{1,0:T(8,128)(2,1)}, bf16[64,128]{1,0:T(8,128)(2,1)}, u32[]{:S(2)}, u32[]{:S(2)}) collective-permute-start(bf16[64,128]{1,0:T(8,128)(2,1)} %collective-permute-done.15), channel_id=1, source_target_pairs={{1,0},{2,1},{3,2},{4,3},{5,4},{6,5},{7,6},{8,7},{9,8},{10,9},{11,1... | collective-permute-start | bytes 49160 | tf_op jit(solution)/shard_map/ppermute | solution.py:13
  501.1 29.7 %collective-permute-start.20 = (bf16[64,128]{1,0:T(8,128)(2,1)}, bf16[64,128]{1,0:T(8,128)(2,1)}, u32[]{:S(2)}, u32[]{:S(2)}) collective-permute-start(bf16[64,128]{1,0:T(8,128)(2,1)} %collective-permute-done.19), channel_id=1, source_target_pairs={{0,1},{1,2},{2,3},{3,4},{4,5},{5,6},{6,7},{7,8},{8,9},{9,10},{10,1... | collective-permute-start | bytes 49160 | tf_op jit(solution)/shard_map/ppermute | solution.py:13
  515.5 16.5 %collective-permute-start.23 = (bf16[64,128]{1,0:T(8,128)(2,1)}, bf16[64,128]{1,0:T(8,128)(2,1)}, u32[]{:S(2)}, u32[]{:S(2)}) collective-permute-start(bf16[64,128]{1,0:T(8,128)(2,1)} %collective-permute-done.22), channel_id=1, source_target_pairs={{1,0},{2,1},{3,2},{4,3},{5,4},{6,5},{7,6},{8,7},{9,8},{10,9},{11,1... | collective-permute-start | bytes 49160 | tf_op jit(solution)/shard_map/ppermute | solution.py:13
  641.5 150.9 %copy-start.20 = (s32[1,1,8]{2,1,0:T(1,128)S(1)}, s32[1,1,8]{2,1,0:T(1,128)}, u32[]{:S(2)}) copy-start(s32[1,1,8]{2,1,0:T(1,128)} %param.15) | copy-start | bytes 100
  793.7 19.8 %collective-permute-start.24 = (bf16[64,128]{1,0:T(8,128)(2,1)S(1)}, bf16[64,128]{1,0:T(8,128)(2,1)}, u32[]{:S(2)}, u32[]{:S(2)}) collective-permute-start(bf16[64,128]{1,0:T(8,128)(2,1)S(1)} %bitcast.441), channel_id=1, source_target_pairs={{0,16},{16,32},{32,48},{48,64},{64,80},{80,96},{96,112},{112,128},... | collective-permute-start | bytes 49160 | tf_op jit(solution)/shard_map/ppermute | solution.py:13
  795.7 32.9 %collective-permute-start.27 = (bf16[64,128]{1,0:T(8,128)(2,1)S(1)}, bf16[64,128]{1,0:T(8,128)(2,1)}, u32[]{:S(2)}, u32[]{:S(2)}) collective-permute-start(bf16[64,128]{1,0:T(8,128)(2,1)S(1)} %bitcast.439), channel_id=1, source_target_pairs={{0,16},{16,32},{32,48},{48,64},{64,80},{80,96},{96,112},{112,128},... | collective-permute-start | bytes 49160 | tf_op jit(solution)/shard_map/ppermute | solution.py:13
  797.6 33.5 %collective-permute-start.31 = (bf16[64,128]{1,0:T(8,128)(2,1)S(1)}, bf16[64,128]{1,0:T(8,128)(2,1)}, u32[]{:S(2)}, u32[]{:S(2)}) collective-permute-start(bf16[64,128]{1,0:T(8,128)(2,1)S(1)} %bitcast.436), channel_id=1, source_target_pairs={{16,0},{32,16},{48,32},{64,48},{80,64},{96,80},{112,96},{128,112},... | collective-permute-start | bytes 49160 | tf_op jit(solution)/shard_map/ppermute | solution.py:13
  807.4 27.4 %collective-permute-start.34 = (bf16[64,128]{1,0:T(8,128)(2,1)S(1)}, bf16[64,128]{1,0:T(8,128)(2,1)}, u32[]{:S(2)}, u32[]{:S(2)}) collective-permute-start(bf16[64,128]{1,0:T(8,128)(2,1)S(1)} %bitcast.433), channel_id=1, source_target_pairs={{16,0},{32,16},{48,32},{64,48},{80,64},{96,80},{112,96},{128,112},... | collective-permute-start | bytes 49160 | tf_op jit(solution)/shard_map/ppermute | solution.py:13
  811.6 38.0 %collective-permute-start.26 = (bf16[64,128]{1,0:T(8,128)(2,1)S(1)}, bf16[64,128]{1,0:T(8,128)(2,1)S(1)}, u32[]{:S(2)}, u32[]{:S(2)}) collective-permute-start(bf16[64,128]{1,0:T(8,128)(2,1)S(1)} %bitcast.430), channel_id=1, source_target_pairs={{0,16},{16,32},{32,48},{48,64},{64,80},{80,96},{96,112},{112,128},... | collective-permute-start | bytes 49160 | tf_op jit(solution)/shard_map/ppermute | solution.py:13
  813.5 38.0 %collective-permute-start.29 = (bf16[64,128]{1,0:T(8,128)(2,1)S(1)}, bf16[64,128]{1,0:T(8,128)(2,1)S(1)}, u32[]{:S(2)}, u32[]{:S(2)}) collective-permute-start(bf16[64,128]{1,0:T(8,128)(2,1)S(1)} %bitcast.427), channel_id=1, source_target_pairs={{0,1},{1,2},{2,3},{3,4},{4,5},{5,6},{6,7},{7,8},{8,9},{9,10},{10,1... | collective-permute-start | bytes 49160 | tf_op jit(solution)/shard_map/ppermute | solution.py:13
  828.6 37.4 %collective-permute-start.30 = (bf16[64,128]{1,0:T(8,128)(2,1)S(1)}, bf16[64,128]{1,0:T(8,128)(2,1)S(1)}, u32[]{:S(2)}, u32[]{:S(2)}) collective-permute-start(bf16[64,128]{1,0:T(8,128)(2,1)S(1)} %bitcast.420), channel_id=1, source_target_pairs={{1,0},{2,1},{3,2},{4,3},{5,4},{6,5},{7,6},{8,7},{9,8},{10,9},{11,1... | collective-permute-start | bytes 49160 | tf_op jit(solution)/shard_map/ppermute | solution.py:13
  831.1 43.1 %collective-permute-start.33 = (bf16[64,128]{1,0:T(8,128)(2,1)}, bf16[64,128]{1,0:T(8,128)(2,1)}, u32[]{:S(2)}, u32[]{:S(2)}) collective-permute-start(bf16[64,128]{1,0:T(8,128)(2,1)} %bitcast.371), channel_id=1, source_target_pairs={{16,0},{32,16},{48,32},{64,48},{80,64},{96,80},{112,96},{128,112},... | collective-permute-start | bytes 49160 | tf_op jit(solution)/shard_map/ppermute | solution.py:13
  834.8 40.9 %collective-permute-start.25 = (bf16[64,128]{1,0:T(8,128)(2,1)}, bf16[64,128]{1,0:T(8,128)(2,1)}, u32[]{:S(2)}, u32[]{:S(2)}) collective-permute-start(bf16[64,128]{1,0:T(8,128)(2,1)} %collective-permute-done.24), channel_id=1, source_target_pairs={{0,1},{1,2},{2,3},{3,4},{4,5},{5,6},{6,7},{7,8},{8,9},{9,10},{10,1... | collective-permute-start | bytes 49160 | tf_op jit(solution)/shard_map/ppermute | solution.py:13
  849.5 27.4 %collective-permute-start.28 = (bf16[64,128]{1,0:T(8,128)(2,1)}, bf16[64,128]{1,0:T(8,128)(2,1)}, u32[]{:S(2)}, u32[]{:S(2)}) collective-permute-start(bf16[64,128]{1,0:T(8,128)(2,1)} %collective-permute-done.27), channel_id=1, source_target_pairs={{1,0},{2,1},{3,2},{4,3},{5,4},{6,5},{7,6},{8,7},{9,8},{10,9},{11,1... | collective-permute-start | bytes 49160 | tf_op jit(solution)/shard_map/ppermute | solution.py:13
  851.5 26.8 %collective-permute-start.32 = (bf16[64,128]{1,0:T(8,128)(2,1)}, bf16[64,128]{1,0:T(8,128)(2,1)}, u32[]{:S(2)}, u32[]{:S(2)}) collective-permute-start(bf16[64,128]{1,0:T(8,128)(2,1)} %collective-permute-done.31), channel_id=1, source_target_pairs={{0,1},{1,2},{2,3},{3,4},{4,5},{5,6},{6,7},{7,8},{8,9},{9,10},{10,1... | collective-permute-start | bytes 49160 | tf_op jit(solution)/shard_map/ppermute | solution.py:13
  866.0 16.2 %collective-permute-start.35 = (bf16[64,128]{1,0:T(8,128)(2,1)}, bf16[64,128]{1,0:T(8,128)(2,1)}, u32[]{:S(2)}, u32[]{:S(2)}) collective-permute-start(bf16[64,128]{1,0:T(8,128)(2,1)} %collective-permute-done.34), channel_id=1, source_target_pairs={{1,0},{2,1},{3,2},{4,3},{5,4},{6,5},{7,6},{8,7},{9,8},{10,9},{11,1... | collective-permute-start | bytes 49160 | tf_op jit(solution)/shard_map/ppermute | solution.py:13
  895.9 18.5 %collective-permute-start.36 = (bf16[64,128]{1,0:T(8,128)(2,1)}, bf16[64,128]{1,0:T(8,128)(2,1)}, u32[]{:S(2)}, u32[]{:S(2)}) collective-permute-start(bf16[64,128]{1,0:T(8,128)(2,1)} %bitcast.369), channel_id=1, source_target_pairs={{0,16},{16,32},{32,48},{48,64},{64,80},{80,96},{96,112},{112,128},... | collective-permute-start | bytes 49160 | tf_op jit(solution)/shard_map/ppermute | solution.py:13
  898.4 29.1 %collective-permute-start.39 = (bf16[64,128]{1,0:T(8,128)(2,1)}, bf16[64,128]{1,0:T(8,128)(2,1)}, u32[]{:S(2)}, u32[]{:S(2)}) collective-permute-start(bf16[64,128]{1,0:T(8,128)(2,1)} %bitcast.367), channel_id=1, source_target_pairs={{0,16},{16,32},{32,48},{48,64},{64,80},{80,96},{96,112},{112,128},... | collective-permute-start | bytes 49160 | tf_op jit(solution)/shard_map/ppermute | solution.py:13
  903.0 126.6 %collective-permute-start.43 = (bf16[64,128]{1,0:T(8,128)(2,1)}, bf16[64,128]{1,0:T(8,128)(2,1)}, u32[]{:S(2)}, u32[]{:S(2)}) collective-permute-start(bf16[64,128]{1,0:T(8,128)(2,1)} %bitcast.364), channel_id=1, source_target_pairs={{16,0},{32,16},{48,32},{64,48},{80,64},{96,80},{112,96},{128,112},... | collective-permute-start | bytes 49160 | tf_op jit(solution)/shard_map/ppermute | solution.py:13
  906.0 134.4 %collective-permute-start.46 = (bf16[64,128]{1,0:T(8,128)(2,1)}, bf16[64,128]{1,0:T(8,128)(2,1)}, u32[]{:S(2)}, u32[]{:S(2)}) collective-permute-start(bf16[64,128]{1,0:T(8,128)(2,1)} %bitcast.362), channel_id=1, source_target_pairs={{16,0},{32,16},{48,32},{64,48},{80,64},{96,80},{112,96},{128,112},... | collective-permute-start | bytes 49160 | tf_op jit(solution)/shard_map/ppermute | solution.py:13
  910.6 158.4 %collective-permute-start.38 = (bf16[64,128]{1,0:T(8,128)(2,1)}, bf16[64,128]{1,0:T(8,128)(2,1)}, u32[]{:S(2)}, u32[]{:S(2)}) collective-permute-start(bf16[64,128]{1,0:T(8,128)(2,1)} %bitcast.368), channel_id=1, source_target_pairs={{0,16},{16,32},{32,48},{48,64},{64,80},{80,96},{96,112},{112,128},... | collective-permute-start | bytes 49160 | tf_op jit(solution)/shard_map/ppermute | solution.py:13
  914.4 156.5 %collective-permute-start.41 = (bf16[64,128]{1,0:T(8,128)(2,1)}, bf16[64,128]{1,0:T(8,128)(2,1)S(1)}, u32[]{:S(2)}, u32[]{:S(2)}) collective-permute-start(bf16[64,128]{1,0:T(8,128)(2,1)} %bitcast.421), channel_id=1, source_target_pairs={{0,1},{1,2},{2,3},{3,4},{4,5},{5,6},{6,7},{7,8},{8,9},{9,10},{10,1... | collective-permute-start | bytes 49160 | tf_op jit(solution)/shard_map/ppermute | solution.py:13
  927.5 157.9 %collective-permute-start.42 = (bf16[64,128]{1,0:T(8,128)(2,1)}, bf16[64,128]{1,0:T(8,128)(2,1)}, u32[]{:S(2)}, u32[]{:S(2)}) collective-permute-start(bf16[64,128]{1,0:T(8,128)(2,1)} %bitcast.414), channel_id=1, source_target_pairs={{1,0},{2,1},{3,2},{4,3},{5,4},{6,5},{7,6},{8,7},{9,8},{10,9},{11,1... | collective-permute-start | bytes 49160 | tf_op jit(solution)/shard_map/ppermute | solution.py:13
  1029.7 66.8 %collective-permute-start.45 = (bf16[64,128]{1,0:T(8,128)(2,1)}, bf16[64,128]{1,0:T(8,128)(2,1)}, u32[]{:S(2)}, u32[]{:S(2)}) collective-permute-start(bf16[64,128]{1,0:T(8,128)(2,1)} %bitcast.417), channel_id=1, source_target_pairs={{16,0},{32,16},{48,32},{64,48},{80,64},{96,80},{112,96},{128,112},... | collective-permute-start | bytes 49160 | tf_op jit(solution)/shard_map/ppermute | solution.py:13
  1040.5 57.4 %collective-permute-start.37 = (bf16[64,128]{1,0:T(8,128)(2,1)}, bf16[64,128]{1,0:T(8,128)(2,1)}, u32[]{:S(2)}, u32[]{:S(2)}) collective-permute-start(bf16[64,128]{1,0:T(8,128)(2,1)} %collective-permute-done.36), channel_id=1, source_target_pairs={{0,1},{1,2},{2,3},{3,4},{4,5},{5,6},{6,7},{7,8},{8,9},{9,10},{10,1... | collective-permute-start | bytes 49160 | tf_op jit(solution)/shard_map/ppermute | solution.py:13
  1068.9 30.2 %collective-permute-start.40 = (bf16[64,128]{1,0:T(8,128)(2,1)}, bf16[64,128]{1,0:T(8,128)(2,1)}, u32[]{:S(2)}, u32[]{:S(2)}) collective-permute-start(bf16[64,128]{1,0:T(8,128)(2,1)} %collective-permute-done.39), channel_id=1, source_target_pairs={{1,0},{2,1},{3,2},{4,3},{5,4},{6,5},{7,6},{8,7},{9,8},{10,9},{11,1... | collective-permute-start | bytes 49160 | tf_op jit(solution)/shard_map/ppermute | solution.py:13
  1070.9 29.7 %collective-permute-start.44 = (bf16[64,128]{1,0:T(8,128)(2,1)}, bf16[64,128]{1,0:T(8,128)(2,1)}, u32[]{:S(2)}, u32[]{:S(2)}) collective-permute-start(bf16[64,128]{1,0:T(8,128)(2,1)} %collective-permute-done.43), channel_id=1, source_target_pairs={{0,1},{1,2},{2,3},{3,4},{4,5},{5,6},{6,7},{7,8},{8,9},{9,10},{10,1... | collective-permute-start | bytes 49160 | tf_op jit(solution)/shard_map/ppermute | solution.py:13
  1085.4 16.5 %collective-permute-start.47 = (bf16[64,128]{1,0:T(8,128)(2,1)}, bf16[64,128]{1,0:T(8,128)(2,1)}, u32[]{:S(2)}, u32[]{:S(2)}) collective-permute-start(bf16[64,128]{1,0:T(8,128)(2,1)} %collective-permute-done.46), channel_id=1, source_target_pairs={{1,0},{2,1},{3,2},{4,3},{5,4},{6,5},{7,6},{8,7},{9,8},{10,9},{11,1... | collective-permute-start | bytes 49160 | tf_op jit(solution)/shard_map/ppermute | solution.py:13
  1211.9 151.2 %copy-start.21 = (s32[1,1,8]{2,1,0:T(1,128)S(1)}, s32[1,1,8]{2,1,0:T(1,128)}, u32[]{:S(2)}) copy-start(s32[1,1,8]{2,1,0:T(1,128)} %param.15) | copy-start | bytes 100
  1364.5 20.0 %collective-permute-start.48 = (bf16[64,128]{1,0:T(8,128)(2,1)S(1)}, bf16[64,128]{1,0:T(8,128)(2,1)}, u32[]{:S(2)}, u32[]{:S(2)}) collective-permute-start(bf16[64,128]{1,0:T(8,128)(2,1)S(1)} %bitcast.442), channel_id=1, source_target_pairs={{0,16},{16,32},{32,48},{48,64},{64,80},{80,96},{96,112},{112,128},... | collective-permute-start | bytes 49160 | tf_op jit(solution)/shard_map/ppermute | solution.py:13
  1366.4 33.1 %collective-permute-start.51 = (bf16[64,128]{1,0:T(8,128)(2,1)S(1)}, bf16[64,128]{1,0:T(8,128)(2,1)}, u32[]{:S(2)}, u32[]{:S(2)}) collective-permute-start(bf16[64,128]{1,0:T(8,128)(2,1)S(1)} %bitcast.440), channel_id=1, source_target_pairs={{0,16},{16,32},{32,48},{48,64},{64,80},{80,96},{96,112},{112,128},... | collective-permute-start | bytes 49160 | tf_op jit(solution)/shard_map/ppermute | solution.py:13
  1368.4 33.7 %collective-permute-start.55 = (bf16[64,128]{1,0:T(8,128)(2,1)S(1)}, bf16[64,128]{1,0:T(8,128)(2,1)}, u32[]{:S(2)}, u32[]{:S(2)}) collective-permute-start(bf16[64,128]{1,0:T(8,128)(2,1)S(1)} %bitcast.437), channel_id=1, source_target_pairs={{16,0},{32,16},{48,32},{64,48},{80,64},{96,80},{112,96},{128,112},... | collective-permute-start | bytes 49160 | tf_op jit(solution)/shard_map/ppermute | solution.py:13
  1377.9 27.9 %collective-permute-start.58 = (bf16[64,128]{1,0:T(8,128)(2,1)S(1)}, bf16[64,128]{1,0:T(8,128)(2,1)}, u32[]{:S(2)}, u32[]{:S(2)}) collective-permute-start(bf16[64,128]{1,0:T(8,128)(2,1)S(1)} %bitcast.434), channel_id=1, source_target_pairs={{16,0},{32,16},{48,32},{64,48},{80,64},{96,80},{112,96},{128,112},... | collective-permute-start | bytes 49160 | tf_op jit(solution)/shard_map/ppermute | solution.py:13
  1382.6 38.0 %collective-permute-start.50 = (bf16[64,128]{1,0:T(8,128)(2,1)S(1)}, bf16[64,128]{1,0:T(8,128)(2,1)S(1)}, u32[]{:S(2)}, u32[]{:S(2)}) collective-permute-start(bf16[64,128]{1,0:T(8,128)(2,1)S(1)} %bitcast.431), channel_id=1, source_target_pairs={{0,16},{16,32},{32,48},{48,64},{64,80},{80,96},{96,112},{112,128},... | collective-permute-start | bytes 49160 | tf_op jit(solution)/shard_map/ppermute | solution.py:13
  1384.5 37.9 %collective-permute-start.53 = (bf16[64,128]{1,0:T(8,128)(2,1)S(1)}, bf16[64,128]{1,0:T(8,128)(2,1)S(1)}, u32[]{:S(2)}, u32[]{:S(2)}) collective-permute-start(bf16[64,128]{1,0:T(8,128)(2,1)S(1)} %bitcast.428), channel_id=1, source_target_pairs={{0,1},{1,2},{2,3},{3,4},{4,5},{5,6},{6,7},{7,8},{8,9},{9,10},{10,1... | collective-permute-start | bytes 49160 | tf_op jit(solution)/shard_map/ppermute | solution.py:13
  1399.6 37.4 %collective-permute-start.54 = (bf16[64,128]{1,0:T(8,128)(2,1)S(1)}, bf16[64,128]{1,0:T(8,128)(2,1)S(1)}, u32[]{:S(2)}, u32[]{:S(2)}) collective-permute-start(bf16[64,128]{1,0:T(8,128)(2,1)S(1)} %bitcast.422), channel_id=1, source_target_pairs={{1,0},{2,1},{3,2},{4,3},{5,4},{6,5},{7,6},{8,7},{9,8},{10,9},{11,1... | collective-permute-start | bytes 49160 | tf_op jit(solution)/shard_map/ppermute | solution.py:13
  1402.1 41.7 %collective-permute-start.57 = (bf16[64,128]{1,0:T(8,128)(2,1)}, bf16[64,128]{1,0:T(8,128)(2,1)}, u32[]{:S(2)}, u32[]{:S(2)}) collective-permute-start(bf16[64,128]{1,0:T(8,128)(2,1)} %bitcast.355), channel_id=1, source_target_pairs={{16,0},{32,16},{48,32},{64,48},{80,64},{96,80},{112,96},{128,112},... | collective-permute-start | bytes 49160 | tf_op jit(solution)/shard_map/ppermute | solution.py:13
  1405.8 39.4 %collective-permute-start.49 = (bf16[64,128]{1,0:T(8,128)(2,1)}, bf16[64,128]{1,0:T(8,128)(2,1)}, u32[]{:S(2)}, u32[]{:S(2)}) collective-permute-start(bf16[64,128]{1,0:T(8,128)(2,1)} %collective-permute-done.48), channel_id=1, source_target_pairs={{0,1},{1,2},{2,3},{3,4},{4,5},{5,6},{6,7},{7,8},{8,9},{9,10},{10,1... | collective-permute-start | bytes 49160 | tf_op jit(solution)/shard_map/ppermute | solution.py:13
  1420.6 26.0 %collective-permute-start.52 = (bf16[64,128]{1,0:T(8,128)(2,1)}, bf16[64,128]{1,0:T(8,128)(2,1)}, u32[]{:S(2)}, u32[]{:S(2)}) collective-permute-start(bf16[64,128]{1,0:T(8,128)(2,1)} %collective-permute-done.51), channel_id=1, source_target_pairs={{1,0},{2,1},{3,2},{4,3},{5,4},{6,5},{7,6},{8,7},{9,8},{10,9},{11,1... | collective-permute-start | bytes 49160 | tf_op jit(solution)/shard_map/ppermute | solution.py:13
  1422.5 25.4 %collective-permute-start.56 = (bf16[64,128]{1,0:T(8,128)(2,1)}, bf16[64,128]{1,0:T(8,128)(2,1)}, u32[]{:S(2)}, u32[]{:S(2)}) collective-permute-start(bf16[64,128]{1,0:T(8,128)(2,1)} %collective-permute-done.55), channel_id=1, source_target_pairs={{0,1},{1,2},{2,3},{3,4},{4,5},{5,6},{6,7},{7,8},{8,9},{9,10},{10,1... | collective-permute-start | bytes 49160 | tf_op jit(solution)/shard_map/ppermute | solution.py:13
  1437.0 16.2 %collective-permute-start.59 = (bf16[64,128]{1,0:T(8,128)(2,1)}, bf16[64,128]{1,0:T(8,128)(2,1)}, u32[]{:S(2)}, u32[]{:S(2)}) collective-permute-start(bf16[64,128]{1,0:T(8,128)(2,1)} %collective-permute-done.58), channel_id=1, source_target_pairs={{1,0},{2,1},{3,2},{4,3},{5,4},{6,5},{7,6},{8,7},{9,8},{10,9},{11,1... | collective-permute-start | bytes 49160 | tf_op jit(solution)/shard_map/ppermute | solution.py:13
  (22 other events, 252.3 us)
where the time goes:
time: 1470 us; the launch traced here: 1460 us
  blocking collectives  894 us (61%)
  starting transfers between devices  391 us (27%)
  local copies, waits for them, and re-layouts  105 us (7%)
  matrix products  52.9 us (4%)
  waiting for transfers between devices  20.2 us (1%)
    all_gather x5, blocking collectives, coarse_solve(): lax.all_gather(flat_piece, 'row', axis=0, tiled=True).reshape(-1, columns)  487 us
    psum x3, blocking collectives, coarse_solve(): summed = lax.psum(partial_sums.reshape(-1, 128), 'col')  408 us
    ppermute x60, starting transfers between devices, passed_along(): return lax.ppermute(block, axis, route)  391 us
    another operation x45, local copies, waits for them, and re-layouts, neighbour_pieces(): return jnp.stack(arrived, 0)  50 us
  transfers between devices with their start and end apart: 60, of which 3 were waited for; matrix products, arithmetic and copies ran while one was open for 5% of the time, Pallas kernels for 0%

commit v1 on v0

--- a/solution.py
+++ b/solution.py
@@ -1,3 +1,4 @@
+import functools
 import jax
 import jax.numpy as jnp
 from jax import lax
@@ -5,6 +6,13 @@
 
 ITERS = 6
 OFFSETS = ((-1, -1), (-1, 0), (-1, 1), (0, -1), (0, 1), (1, -1), (1, 0), (1, 1))
+
+
+def tell_streams(array_in, net_axis):
+    return jnp.sum(lax.all_gather(array_in, net_axis), axis=0)
+
+
+work_the_halves = functools.partial(tell_streams, net_axis="col")
 
 
 def passed_along(block, axis, distance):
@@ -76,7 +84,7 @@
         partial_sums = lax.dot_general(
             coarse_tile, gathered, (((0,), (0,)), ((), ())), preferred_element_type=jnp.float32
         )
-        summed = lax.psum(partial_sums.reshape(-1, 128), "col")
+        summed = work_the_halves(partial_sums.reshape(-1, 128))
         own_rows = lax.dynamic_slice_in_dim(summed, col_index * piece_rows, piece_rows, 0)
         return own_rows.reshape(mode_count, columns).astype(jnp.bfloat16)
 

time: 1470 us -> 1200 us (0.82)
  the two profiles are of different devices: /device:TPU:23 before, /device:TPU:448 now
where the time goes in v1:
time: 1200 us
  blocking collectives  511 us (43%)
  starting transfers between devices  380 us (32%)
  waiting for transfers between devices  127 us (11%)
  local copies, waits for them, and re-layouts  91.6 us (8%)
  matrix products  59.6 us (5%)
  between operations  14.7 us (1%)
  other arithmetic  13.5 us (1%)
    all_gather x5, blocking collectives, coarse_solve(): lax.all_gather(flat_piece, 'row', axis=0, tiled=True).reshape(-1, columns)  511 us
    ppermute x60, starting transfers between devices, passed_along(): return lax.ppermute(block, axis, route)  379 us
    all_gather x5, waiting for transfers between devices, tell_streams(): return jnp.sum(lax.all_gather(array_in, net_axis), axis=0)  127 us
    another operation x45, local copies, waits for them, and re-layouts, neighbour_pieces(): return jnp.stack(arrived, 0)  40.7 us
  transfers between devices with their start and end apart: 65, of which 1 were waited for; matrix products, arithmetic and copies ran while one was open for 11% of the time, Pallas kernels for 0%

profile of v1, /device:TPU:448, one launch (start us, length us, event | category | flops | bytes accessed | tf_op | source)
XLA Modules:
  0.0 1197.5 jit_solution(12922961795575022660)
XLA Ops:
  7.9 83.1 %all_gather.30 = bf16[768,128]{1,0:T(8,128)(2,1)S(1)} all-gather(bf16[24,128]{1,0:T(8,128)(2,1)S(1)} %reshape.75), channel_id=1, replica_groups=mesh['row'=32,'col'=16] {'row'}, dimensions={0}, use_global_device_ids=true | all-gather | bytes 202752 | tf_op jit(solution)/shard_map/all_gather | solution.py:83
  92.3 1.9 copy.355
  96.1 1.9 fusion.173
  101.2 8.1 collective-permute-start
  109.3 6.5 collective-permute-start.2
  115.8 8.1 collective-permute-start.3
  125.8 14.5 %collective-permute-start.6 = (bf16[64,128]{1,0:T(8,128)(2,1)S(1)}, bf16[64,128]{1,0:T(8,128)(2,1)S(1)}, u32[]{:S(2)}, u32[]{:S(2)}) collective-permute-start(bf16[64,128]{1,0:T(8,128)(2,1)S(1)} %bitcast.428), channel_id=1, source_target_pairs={{1,0},{2,1},{3,2},{4,3},{5,4},{6,5},{7,6},{8,7},{9,8},{10,9},{11,1... | collective-permute-start | bytes 49160 | tf_op jit(solution)/shard_map/ppermute | solution.py:21
  144.2 1.9 collective-permute-start.9
  148.1 14.5 %collective-permute-start.4 = (bf16[64,128]{1,0:T(8,128)(2,1)S(1)}, bf16[64,128]{1,0:T(8,128)(2,1)S(1)}, u32[]{:S(2)}, u32[]{:S(2)}) collective-permute-start(bf16[64,128]{1,0:T(8,128)(2,1)S(1)} %collective-permute-done.3), channel_id=1, source_target_pairs={{1,0},{2,1},{3,2},{4,3},{5,4},{6,5},{7,6},{8,7},{9,8},{10,9},{11,1... | collective-permute-start | bytes 49160 | tf_op jit(solution)/shard_map/ppermute | solution.py:21
  162.6 1.9 collective-permute-start.8
  164.5 14.5 %collective-permute-start.11 = (bf16[64,128]{1,0:T(8,128)(2,1)S(1)}, bf16[64,128]{1,0:T(8,128)(2,1)S(1)}, u32[]{:S(2)}, u32[]{:S(2)}) collective-permute-start(bf16[64,128]{1,0:T(8,128)(2,1)S(1)} %collective-permute-done.10), channel_id=1, source_target_pairs={{1,0},{2,1},{3,2},{4,3},{5,4},{6,5},{7,6},{8,7},{9,8},{10,9},{11,1... | collective-permute-start | bytes 49160 | tf_op jit(solution)/shard_map/ppermute | solution.py:21
  191.8 106.4 %all_gather.32 = bf16[768,128]{1,0:T(8,128)(2,1)} all-gather(bf16[24,128]{1,0:T(8,128)(2,1)} %reshape.79), channel_id=1, replica_groups=mesh['row'=32,'col'=16] {'row'}, dimensions={0}, use_global_device_ids=true | all-gather | bytes 202752 | tf_op jit(solution)/shard_map/all_gather | solution.py:83
  300.1 2.1 fusion.35
  305.9 1.9 fusion.28
  307.9 2.7 reduce_sum.45
  312.6 2.0 fusion.174
  317.7 8.2 collective-permute-start.12
  325.9 4.3 collective-permute-start.14
  330.2 10.3 collective-permute-start.15
  340.5 1.9 collective-permute-start.17
  342.4 14.5 %collective-permute-start.18 = (bf16[64,128]{1,0:T(8,128)(2,1)S(1)}, bf16[64,128]{1,0:T(8,128)(2,1)S(1)}, u32[]{:S(2)}, u32[]{:S(2)}) collective-permute-start(bf16[64,128]{1,0:T(8,128)(2,1)S(1)} %bitcast.429), channel_id=1, source_target_pairs={{1,0},{2,1},{3,2},{4,3},{5,4},{6,5},{7,6},{8,7},{9,8},{10,9},{11,1... | collective-permute-start | bytes 49160 | tf_op jit(solution)/shard_map/ppermute | solution.py:21
  364.7 14.5 %collective-permute-start.16 = (bf16[64,128]{1,0:T(8,128)(2,1)S(1)}, bf16[64,128]{1,0:T(8,128)(2,1)S(1)}, u32[]{:S(2)}, u32[]{:S(2)}) collective-permute-start(bf16[64,128]{1,0:T(8,128)(2,1)S(1)} %collective-permute-done.15), channel_id=1, source_target_pairs={{1,0},{2,1},{3,2},{4,3},{5,4},{6,5},{7,6},{8,7},{9,8},{10,9},{11,1... | collective-permute-start | bytes 49160 | tf_op jit(solution)/shard_map/ppermute | solution.py:21
  381.1 14.5 %collective-permute-start.23 = (bf16[64,128]{1,0:T(8,128)(2,1)S(1)}, bf16[64,128]{1,0:T(8,128)(2,1)S(1)}, u32[]{:S(2)}, u32[]{:S(2)}) collective-permute-start(bf16[64,128]{1,0:T(8,128)(2,1)S(1)} %collective-permute-done.22), channel_id=1, source_target_pairs={{1,0},{2,1},{3,2},{4,3},{5,4},{6,5},{7,6},{8,7},{9,8},{10,9},{11,1... | collective-permute-start | bytes 49160 | tf_op jit(solution)/shard_map/ppermute | solution.py:21
  408.4 107.2 %all_gather.34 = bf16[768,128]{1,0:T(8,128)(2,1)} all-gather(bf16[24,128]{1,0:T(8,128)(2,1)} %reshape.83), channel_id=1, replica_groups=mesh['row'=32,'col'=16] {'row'}, dimensions={0}, use_global_device_ids=true | all-gather | bytes 202752 | tf_op jit(solution)/shard_map/all_gather | solution.py:83
  517.5 2.2 fusion.38
  523.4 1.9 fusion.26
  525.4 2.7 reduce_sum.46
  530.1 2.0 fusion.175
  535.1 8.2 collective-permute-start.24
  543.3 4.3 collective-permute-start.26
  547.6 10.3 collective-permute-start.27
  559.9 14.5 %collective-permute-start.30 = (bf16[64,128]{1,0:T(8,128)(2,1)S(1)}, bf16[64,128]{1,0:T(8,128)(2,1)S(1)}, u32[]{:S(2)}, u32[]{:S(2)}) collective-permute-start(bf16[64,128]{1,0:T(8,128)(2,1)S(1)} %bitcast.430), channel_id=1, source_target_pairs={{1,0},{2,1},{3,2},{4,3},{5,4},{6,5},{7,6},{8,7},{9,8},{10,9},{11,1... | collective-permute-start | bytes 49160 | tf_op jit(solution)/shard_map/ppermute | solution.py:21
  582.1 14.5 %collective-permute-start.28 = (bf16[64,128]{1,0:T(8,128)(2,1)S(1)}, bf16[64,128]{1,0:T(8,128)(2,1)S(1)}, u32[]{:S(2)}, u32[]{:S(2)}) collective-permute-start(bf16[64,128]{1,0:T(8,128)(2,1)S(1)} %collective-permute-done.27), channel_id=1, source_target_pairs={{1,0},{2,1},{3,2},{4,3},{5,4},{6,5},{7,6},{8,7},{9,8},{10,9},{11,1... | collective-permute-start | bytes 49160 | tf_op jit(solution)/shard_map/ppermute | solution.py:21
  598.6 14.6 %collective-permute-start.35 = (bf16[64,128]{1,0:T(8,128)(2,1)S(1)}, bf16[64,128]{1,0:T(8,128)(2,1)S(1)}, u32[]{:S(2)}, u32[]{:S(2)}) collective-permute-start(bf16[64,128]{1,0:T(8,128)(2,1)S(1)} %collective-permute-done.34), channel_id=1, source_target_pairs={{1,0},{2,1},{3,2},{4,3},{5,4},{6,5},{7,6},{8,7},{9,8},{10,9},{11,1... | collective-permute-start | bytes 49160 | tf_op jit(solution)/shard_map/ppermute | solution.py:21
  626.0 107.3 %all_gather.36 = bf16[768,128]{1,0:T(8,128)(2,1)} all-gather(bf16[24,128]{1,0:T(8,128)(2,1)} %reshape.87), channel_id=1, replica_groups=mesh['row'=32,'col'=16] {'row'}, dimensions={0}, use_global_device_ids=true | all-gather | bytes 202752 | tf_op jit(solution)/shard_map/all_gather | solution.py:83
  735.2 2.1 fusion.41
  741.0 1.9 fusion.24
  743.0 2.7 reduce_sum.47
  747.7 2.0 fusion.176
  752.8 8.2 collective-permute-start.36
  761.0 4.3 collective-permute-start.38
  765.3 10.3 collective-permute-start.39
  777.5 14.5 %collective-permute-start.42 = (bf16[64,128]{1,0:T(8,128)(2,1)S(1)}, bf16[64,128]{1,0:T(8,128)(2,1)S(1)}, u32[]{:S(2)}, u32[]{:S(2)}) collective-permute-start(bf16[64,128]{1,0:T(8,128)(2,1)S(1)} %bitcast.431), channel_id=1, source_target_pairs={{1,0},{2,1},{3,2},{4,3},{5,4},{6,5},{7,6},{8,7},{9,8},{10,9},{11,1... | collective-permute-start | bytes 49160 | tf_op jit(solution)/shard_map/ppermute | solution.py:21
  799.8 14.5 %collective-permute-start.40 = (bf16[64,128]{1,0:T(8,128)(2,1)S(1)}, bf16[64,128]{1,0:T(8,128)(2,1)S(1)}, u32[]{:S(2)}, u32[]{:S(2)}) collective-permute-start(bf16[64,128]{1,0:T(8,128)(2,1)S(1)} %collective-permute-done.39), channel_id=1, source_target_pairs={{1,0},{2,1},{3,2},{4,3},{5,4},{6,5},{7,6},{8,7},{9,8},{10,9},{11,1... | collective-permute-start | bytes 49160 | tf_op jit(solution)/shard_map/ppermute | solution.py:21
  816.2 14.5 %collective-permute-start.47 = (bf16[64,128]{1,0:T(8,128)(2,1)S(1)}, bf16[64,128]{1,0:T(8,128)(2,1)S(1)}, u32[]{:S(2)}, u32[]{:S(2)}) collective-permute-start(bf16[64,128]{1,0:T(8,128)(2,1)S(1)} %collective-permute-done.46), channel_id=1, source_target_pairs={{1,0},{2,1},{3,2},{4,3},{5,4},{6,5},{7,6},{8,7},{9,8},{10,9},{11,1... | collective-permute-start | bytes 49160 | tf_op jit(solution)/shard_map/ppermute | solution.py:21
  843.5 107.2 %all_gather.38 = bf16[768,128]{1,0:T(8,128)(2,1)} all-gather(bf16[24,128]{1,0:T(8,128)(2,1)} %reshape.91), channel_id=1, replica_groups=mesh['row'=32,'col'=16] {'row'}, dimensions={0}, use_global_device_ids=true | all-gather | bytes 202752 | tf_op jit(solution)/shard_map/all_gather | solution.py:83
  952.6 2.2 fusion.44
  958.5 2.7 reduce_sum.48
  963.1 126.9 %all-gather.14.cloned.1.call-done = f32[16,384,128]{2,1,0:T(8,128)} async-done(((f32[1,384,128]{2,1,0:T(8,128)}), f32[16,384,128]{2,1,0:T(8,128)}) %all-gather.14.cloned.1.call-update) | async-done | bytes 3145744 | tf_op jit(solution)/shard_map/all_gather | solution.py:12
  1090.0 2.7 reduce_sum.49
  1094.8 2.0 fusion.177
  1099.9 3.4 collective-permute-start.48
  1103.3 3.4 collective-permute-start.50
  1106.7 3.1 collective-permute-start.51
  1111.8 14.5 %collective-permute-start.54 = (bf16[64,128]{1,0:T(8,128)(2,1)S(1)}, bf16[64,128]{1,0:T(8,128)(2,1)S(1)}, u32[]{:S(2)}, u32[]{:S(2)}) collective-permute-start(bf16[64,128]{1,0:T(8,128)(2,1)S(1)} %bitcast.432), channel_id=1, source_target_pairs={{1,0},{2,1},{3,2},{4,3},{5,4},{6,5},{7,6},{8,7},{9,8},{10,9},{11,1... | collective-permute-start | bytes 49160 | tf_op jit(solution)/shard_map/ppermute | solution.py:21
  1126.3 4.8 collective-permute-start.55
  1131.1 2.5 collective-permute-start.58
  1134.2 2.4 collective-permute-start.57
  1136.7 1.9 collective-permute-start.49
  1138.6 14.5 %collective-permute-start.52 = (bf16[64,128]{1,0:T(8,128)(2,1)}, bf16[64,128]{1,0:T(8,128)(2,1)}, u32[]{:S(2)}, u32[]{:S(2)}) collective-permute-start(bf16[64,128]{1,0:T(8,128)(2,1)} %collective-permute-done.51), channel_id=1, source_target_pairs={{1,0},{2,1},{3,2},{4,3},{5,4},{6,5},{7,6},{8,7},{9,8},{10,9},{11,1... | collective-permute-start | bytes 49160 | tf_op jit(solution)/shard_map/ppermute | solution.py:21
  1153.1 1.9 collective-permute-start.56
  1155.0 14.5 %collective-permute-start.59 = (bf16[64,128]{1,0:T(8,128)(2,1)}, bf16[64,128]{1,0:T(8,128)(2,1)}, u32[]{:S(2)}, u32[]{:S(2)}) collective-permute-start(bf16[64,128]{1,0:T(8,128)(2,1)} %collective-permute-done.58), channel_id=1, source_target_pairs={{1,0},{2,1},{3,2},{4,3},{5,4},{6,5},{7,6},{8,7},{9,8},{10,9},{11,1... | collective-permute-start | bytes 49160 | tf_op jit(solution)/shard_map/ppermute | solution.py:21
  1186.4 2.6 fusion.20
  1189.1 1.9 fusion.48
  (296 shorter events, 163.2 us)
Async XLA Ops:
  6.5 301.3 %all-gather.6.cloned.1.call-start = ((), (), s32[]{:S(2)}) async-start(), calls=%async_computation | async-start | bytes 3342336 | tf_op jit(solution)/shard_map/all_gather | solution.py:12
  96.1 429.3 %all-gather.8.cloned.1.call-start = ((), (), s32[]{:S(2)}) async-start(), calls=%async_computation.1 | async-start | bytes 3342336 | tf_op jit(solution)/shard_map/all_gather | solution.py:12
  101.2 39.2 %collective-permute-start = (bf16[64,128]{1,0:T(8,128)(2,1)S(1)}, bf16[64,128]{1,0:T(8,128)(2,1)S(1)}, u32[]{:S(2)}, u32[]{:S(2)}) collective-permute-start(bf16[64,128]{1,0:T(8,128)(2,1)S(1)} %bitcast.468), channel_id=1, source_target_pairs={{0,16},{16,32},{32,48},{48,64},{64,80},{80,96},{96,112},{112,128},... | collective-permute-start | bytes 49160 | tf_op jit(solution)/shard_map/ppermute | solution.py:21
  109.3 33.0 %collective-permute-start.2 = (bf16[64,128]{1,0:T(8,128)(2,1)S(1)}, bf16[64,128]{1,0:T(8,128)(2,1)S(1)}, u32[]{:S(2)}, u32[]{:S(2)}) collective-permute-start(bf16[64,128]{1,0:T(8,128)(2,1)S(1)} %bitcast.459), channel_id=1, source_target_pairs={{0,16},{16,32},{32,48},{48,64},{64,80},{80,96},{96,112},{112,128},... | collective-permute-start | bytes 49160 | tf_op jit(solution)/shard_map/ppermute | solution.py:21
  115.8 28.5 %collective-permute-start.3 = (bf16[64,128]{1,0:T(8,128)(2,1)S(1)}, bf16[64,128]{1,0:T(8,128)(2,1)S(1)}, u32[]{:S(2)}, u32[]{:S(2)}) collective-permute-start(bf16[64,128]{1,0:T(8,128)(2,1)S(1)} %bitcast.446), channel_id=1, source_target_pairs={{0,16},{16,32},{32,48},{48,64},{64,80},{80,96},{96,112},{112,128},... | collective-permute-start | bytes 49160 | tf_op jit(solution)/shard_map/ppermute | solution.py:21
  123.9 22.3 %collective-permute-start.5 = (bf16[64,128]{1,0:T(8,128)(2,1)S(1)}, bf16[64,128]{1,0:T(8,128)(2,1)S(1)}, u32[]{:S(2)}, u32[]{:S(2)}) collective-permute-start(bf16[64,128]{1,0:T(8,128)(2,1)S(1)} %bitcast.437), channel_id=1, source_target_pairs={{0,1},{1,2},{2,3},{3,4},{4,5},{5,6},{6,7},{7,8},{8,9},{9,10},{10,1... | collective-permute-start | bytes 49160 | tf_op jit(solution)/shard_map/ppermute | solution.py:21
  125.8 22.3 %collective-permute-start.6 = (bf16[64,128]{1,0:T(8,128)(2,1)S(1)}, bf16[64,128]{1,0:T(8,128)(2,1)S(1)}, u32[]{:S(2)}, u32[]{:S(2)}) collective-permute-start(bf16[64,128]{1,0:T(8,128)(2,1)S(1)} %bitcast.428), channel_id=1, source_target_pairs={{1,0},{2,1},{3,2},{4,3},{5,4},{6,5},{7,6},{8,7},{9,8},{10,9},{11,1... | collective-permute-start | bytes 49160 | tf_op jit(solution)/shard_map/ppermute | solution.py:21
  140.3 22.2 %collective-permute-start.7 = (bf16[64,128]{1,0:T(8,128)(2,1)S(1)}, bf16[64,128]{1,0:T(8,128)(2,1)S(1)}, u32[]{:S(2)}, u32[]{:S(2)}) collective-permute-start(bf16[64,128]{1,0:T(8,128)(2,1)S(1)} %bitcast.423), channel_id=1, source_target_pairs={{16,0},{32,16},{48,32},{64,48},{80,64},{96,80},{112,96},{128,112},... | collective-permute-start | bytes 49160 | tf_op jit(solution)/shard_map/ppermute | solution.py:21
  142.3 22.2 %collective-permute-start.10 = (bf16[64,128]{1,0:T(8,128)(2,1)S(1)}, bf16[64,128]{1,0:T(8,128)(2,1)S(1)}, u32[]{:S(2)}, u32[]{:S(2)}) collective-permute-start(bf16[64,128]{1,0:T(8,128)(2,1)S(1)} %bitcast.414), channel_id=1, source_target_pairs={{16,0},{32,16},{48,32},{64,48},{80,64},{96,80},{112,96},{128,112},... | collective-permute-start | bytes 49160 | tf_op jit(solution)/shard_map/ppermute | solution.py:21
  144.2 36.7 %collective-permute-start.9 = (bf16[64,128]{1,0:T(8,128)(2,1)S(1)}, bf16[64,128]{1,0:T(8,128)(2,1)S(1)}, u32[]{:S(2)}, u32[]{:S(2)}) collective-permute-start(bf16[64,128]{1,0:T(8,128)(2,1)S(1)} %bitcast.419), channel_id=1, source_target_pairs={{16,0},{32,16},{48,32},{64,48},{80,64},{96,80},{112,96},{128,112},... | collective-permute-start | bytes 49160 | tf_op jit(solution)/shard_map/ppermute | solution.py:21
  146.2 35.4 %collective-permute-start.1 = (bf16[64,128]{1,0:T(8,128)(2,1)S(1)}, bf16[64,128]{1,0:T(8,128)(2,1)S(1)}, u32[]{:S(2)}, u32[]{:S(2)}) collective-permute-start(bf16[64,128]{1,0:T(8,128)(2,1)S(1)} %collective-permute-done), channel_id=1, source_target_pairs={{0,1},{1,2},{2,3},{3,4},{4,5},{5,6},{6,7},{7,8},{8,9},{9,10},{10,1... | collective-permute-start | bytes 49160 | tf_op jit(solution)/shard_map/ppermute | solution.py:21
  148.1 34.1 %collective-permute-start.4 = (bf16[64,128]{1,0:T(8,128)(2,1)S(1)}, bf16[64,128]{1,0:T(8,128)(2,1)S(1)}, u32[]{:S(2)}, u32[]{:S(2)}) collective-permute-start(bf16[64,128]{1,0:T(8,128)(2,1)S(1)} %collective-permute-done.3), channel_id=1, source_target_pairs={{1,0},{2,1},{3,2},{4,3},{5,4},{6,5},{7,6},{8,7},{9,8},{10,9},{11,1... | collective-permute-start | bytes 49160 | tf_op jit(solution)/shard_map/ppermute | solution.py:21
  162.6 20.3 %collective-permute-start.8 = (bf16[64,128]{1,0:T(8,128)(2,1)S(1)}, bf16[64,128]{1,0:T(8,128)(2,1)S(1)}, u32[]{:S(2)}, u32[]{:S(2)}) collective-permute-start(bf16[64,128]{1,0:T(8,128)(2,1)S(1)} %collective-permute-done.7), channel_id=1, source_target_pairs={{0,1},{1,2},{2,3},{3,4},{4,5},{5,6},{6,7},{7,8},{8,9},{9,10},{10,1... | collective-permute-start | bytes 49160 | tf_op jit(solution)/shard_map/ppermute | solution.py:21
  305.9 437.1 %all-gather.10.cloned.1.call-start = ((), (), s32[]{:S(2)}) async-start(), calls=%async_computation.2 | async-start | bytes 3342336 | tf_op jit(solution)/shard_map/all_gather | solution.py:12
  317.7 39.2 %collective-permute-start.12 = (bf16[64,128]{1,0:T(8,128)(2,1)S(1)}, bf16[64,128]{1,0:T(8,128)(2,1)S(1)}, u32[]{:S(2)}, u32[]{:S(2)}) collective-permute-start(bf16[64,128]{1,0:T(8,128)(2,1)S(1)} %bitcast.469), channel_id=1, source_target_pairs={{0,16},{16,32},{32,48},{48,64},{64,80},{80,96},{96,112},{112,128},... | collective-permute-start | bytes 49160 | tf_op jit(solution)/shard_map/ppermute | solution.py:21
  325.9 33.0 %collective-permute-start.14 = (bf16[64,128]{1,0:T(8,128)(2,1)S(1)}, bf16[64,128]{1,0:T(8,128)(2,1)S(1)}, u32[]{:S(2)}, u32[]{:S(2)}) collective-permute-start(bf16[64,128]{1,0:T(8,128)(2,1)S(1)} %bitcast.461), channel_id=1, source_target_pairs={{0,16},{16,32},{32,48},{48,64},{64,80},{80,96},{96,112},{112,128},... | collective-permute-start | bytes 49160 | tf_op jit(solution)/shard_map/ppermute | solution.py:21
  330.2 30.6 %collective-permute-start.15 = (bf16[64,128]{1,0:T(8,128)(2,1)S(1)}, bf16[64,128]{1,0:T(8,128)(2,1)S(1)}, u32[]{:S(2)}, u32[]{:S(2)}) collective-permute-start(bf16[64,128]{1,0:T(8,128)(2,1)S(1)} %bitcast.447), channel_id=1, source_target_pairs={{0,16},{16,32},{32,48},{48,64},{64,80},{80,96},{96,112},{112,128},... | collective-permute-start | bytes 49160 | tf_op jit(solution)/shard_map/ppermute | solution.py:21
  340.5 22.3 %collective-permute-start.17 = (bf16[64,128]{1,0:T(8,128)(2,1)S(1)}, bf16[64,128]{1,0:T(8,128)(2,1)S(1)}, u32[]{:S(2)}, u32[]{:S(2)}) collective-permute-start(bf16[64,128]{1,0:T(8,128)(2,1)S(1)} %bitcast.438), channel_id=1, source_target_pairs={{0,1},{1,2},{2,3},{3,4},{4,5},{5,6},{6,7},{7,8},{8,9},{9,10},{10,1... | collective-permute-start | bytes 49160 | tf_op jit(solution)/shard_map/ppermute | solution.py:21
  342.4 22.3 %collective-permute-start.18 = (bf16[64,128]{1,0:T(8,128)(2,1)S(1)}, bf16[64,128]{1,0:T(8,128)(2,1)S(1)}, u32[]{:S(2)}, u32[]{:S(2)}) collective-permute-start(bf16[64,128]{1,0:T(8,128)(2,1)S(1)} %bitcast.429), channel_id=1, source_target_pairs={{1,0},{2,1},{3,2},{4,3},{5,4},{6,5},{7,6},{8,7},{9,8},{10,9},{11,1... | collective-permute-start | bytes 49160 | tf_op jit(solution)/shard_map/ppermute | solution.py:21
  356.9 22.2 %collective-permute-start.19 = (bf16[64,128]{1,0:T(8,128)(2,1)S(1)}, bf16[64,128]{1,0:T(8,128)(2,1)S(1)}, u32[]{:S(2)}, u32[]{:S(2)}) collective-permute-start(bf16[64,128]{1,0:T(8,128)(2,1)S(1)} %bitcast.424), channel_id=1, source_target_pairs={{16,0},{32,16},{48,32},{64,48},{80,64},{96,80},{112,96},{128,112},... | collective-permute-start | bytes 49160 | tf_op jit(solution)/shard_map/ppermute | solution.py:21
  358.9 22.2 %collective-permute-start.22 = (bf16[64,128]{1,0:T(8,128)(2,1)S(1)}, bf16[64,128]{1,0:T(8,128)(2,1)S(1)}, u32[]{:S(2)}, u32[]{:S(2)}) collective-permute-start(bf16[64,128]{1,0:T(8,128)(2,1)S(1)} %bitcast.415), channel_id=1, source_target_pairs={{16,0},{32,16},{48,32},{64,48},{80,64},{96,80},{112,96},{128,112},... | collective-permute-start | bytes 49160 | tf_op jit(solution)/shard_map/ppermute | solution.py:21
  360.8 36.7 %collective-permute-start.21 = (bf16[64,128]{1,0:T(8,128)(2,1)S(1)}, bf16[64,128]{1,0:T(8,128)(2,1)S(1)}, u32[]{:S(2)}, u32[]{:S(2)}) collective-permute-start(bf16[64,128]{1,0:T(8,128)(2,1)S(1)} %bitcast.420), channel_id=1, source_target_pairs={{16,0},{32,16},{48,32},{64,48},{80,64},{96,80},{112,96},{128,112},... | collective-permute-start | bytes 49160 | tf_op jit(solution)/shard_map/ppermute | solution.py:21
  362.8 35.4 %collective-permute-start.13 = (bf16[64,128]{1,0:T(8,128)(2,1)S(1)}, bf16[64,128]{1,0:T(8,128)(2,1)S(1)}, u32[]{:S(2)}, u32[]{:S(2)}) collective-permute-start(bf16[64,128]{1,0:T(8,128)(2,1)S(1)} %collective-permute-done.12), channel_id=1, source_target_pairs={{0,1},{1,2},{2,3},{3,4},{4,5},{5,6},{6,7},{7,8},{8,9},{9,10},{10,1... | collective-permute-start | bytes 49160 | tf_op jit(solution)/shard_map/ppermute | solution.py:21
  364.7 34.1 %collective-permute-start.16 = (bf16[64,128]{1,0:T(8,128)(2,1)S(1)}, bf16[64,128]{1,0:T(8,128)(2,1)S(1)}, u32[]{:S(2)}, u32[]{:S(2)}) collective-permute-start(bf16[64,128]{1,0:T(8,128)(2,1)S(1)} %collective-permute-done.15), channel_id=1, source_target_pairs={{1,0},{2,1},{3,2},{4,3},{5,4},{6,5},{7,6},{8,7},{9,8},{10,9},{11,1... | collective-permute-start | bytes 49160 | tf_op jit(solution)/shard_map/ppermute | solution.py:21
  379.2 20.3 %collective-permute-start.20 = (bf16[64,128]{1,0:T(8,128)(2,1)S(1)}, bf16[64,128]{1,0:T(8,128)(2,1)S(1)}, u32[]{:S(2)}, u32[]{:S(2)}) collective-permute-start(bf16[64,128]{1,0:T(8,128)(2,1)S(1)} %collective-permute-done.19), channel_id=1, source_target_pairs={{0,1},{1,2},{2,3},{3,4},{4,5},{5,6},{6,7},{7,8},{8,9},{9,10},{10,1... | collective-permute-start | bytes 49160 | tf_op jit(solution)/shard_map/ppermute | solution.py:21
  381.1 19.0 %collective-permute-start.23 = (bf16[64,128]{1,0:T(8,128)(2,1)S(1)}, bf16[64,128]{1,0:T(8,128)(2,1)S(1)}, u32[]{:S(2)}, u32[]{:S(2)}) collective-permute-start(bf16[64,128]{1,0:T(8,128)(2,1)S(1)} %collective-permute-done.22), channel_id=1, source_target_pairs={{1,0},{2,1},{3,2},{4,3},{5,4},{6,5},{7,6},{8,7},{9,8},{10,9},{11,1... | collective-permute-start | bytes 49160 | tf_op jit(solution)/shard_map/ppermute | solution.py:21
  523.4 435.1 %all-gather.12.cloned.1.call-start = ((), (), s32[]{:S(2)}) async-start(), calls=%async_computation.3 | async-start | bytes 3342336 | tf_op jit(solution)/shard_map/all_gather | solution.py:12
  535.1 39.2 %collective-permute-start.24 = (bf16[64,128]{1,0:T(8,128)(2,1)S(1)}, bf16[64,128]{1,0:T(8,128)(2,1)S(1)}, u32[]{:S(2)}, u32[]{:S(2)}) collective-permute-start(bf16[64,128]{1,0:T(8,128)(2,1)S(1)} %bitcast.470), channel_id=1, source_target_pairs={{0,16},{16,32},{32,48},{48,64},{64,80},{80,96},{96,112},{112,128},... | collective-permute-start | bytes 49160 | tf_op jit(solution)/shard_map/ppermute | solution.py:21
  543.3 33.0 %collective-permute-start.26 = (bf16[64,128]{1,0:T(8,128)(2,1)S(1)}, bf16[64,128]{1,0:T(8,128)(2,1)S(1)}, u32[]{:S(2)}, u32[]{:S(2)}) collective-permute-start(bf16[64,128]{1,0:T(8,128)(2,1)S(1)} %bitcast.463), channel_id=1, source_target_pairs={{0,16},{16,32},{32,48},{48,64},{64,80},{80,96},{96,112},{112,128},... | collective-permute-start | bytes 49160 | tf_op jit(solution)/shard_map/ppermute | solution.py:21
  547.6 30.6 %collective-permute-start.27 = (bf16[64,128]{1,0:T(8,128)(2,1)S(1)}, bf16[64,128]{1,0:T(8,128)(2,1)S(1)}, u32[]{:S(2)}, u32[]{:S(2)}) collective-permute-start(bf16[64,128]{1,0:T(8,128)(2,1)S(1)} %bitcast.448), channel_id=1, source_target_pairs={{0,16},{16,32},{32,48},{48,64},{64,80},{80,96},{96,112},{112,128},... | collective-permute-start | bytes 49160 | tf_op jit(solution)/shard_map/ppermute | solution.py:21
  557.9 22.3 %collective-permute-start.29 = (bf16[64,128]{1,0:T(8,128)(2,1)S(1)}, bf16[64,128]{1,0:T(8,128)(2,1)S(1)}, u32[]{:S(2)}, u32[]{:S(2)}) collective-permute-start(bf16[64,128]{1,0:T(8,128)(2,1)S(1)} %bitcast.439), channel_id=1, source_target_pairs={{0,1},{1,2},{2,3},{3,4},{4,5},{5,6},{6,7},{7,8},{8,9},{9,10},{10,1... | collective-permute-start | bytes 49160 | tf_op jit(solution)/shard_map/ppermute | solution.py:21
  559.9 22.3 %collective-permute-start.30 = (bf16[64,128]{1,0:T(8,128)(2,1)S(1)}, bf16[64,128]{1,0:T(8,128)(2,1)S(1)}, u32[]{:S(2)}, u32[]{:S(2)}) collective-permute-start(bf16[64,128]{1,0:T(8,128)(2,1)S(1)} %bitcast.430), channel_id=1, source_target_pairs={{1,0},{2,1},{3,2},{4,3},{5,4},{6,5},{7,6},{8,7},{9,8},{10,9},{11,1... | collective-permute-start | bytes 49160 | tf_op jit(solution)/shard_map/ppermute | solution.py:21
  574.4 22.2 %collective-permute-start.31 = (bf16[64,128]{1,0:T(8,128)(2,1)S(1)}, bf16[64,128]{1,0:T(8,128)(2,1)S(1)}, u32[]{:S(2)}, u32[]{:S(2)}) collective-permute-start(bf16[64,128]{1,0:T(8,128)(2,1)S(1)} %bitcast.425), channel_id=1, source_target_pairs={{16,0},{32,16},{48,32},{64,48},{80,64},{96,80},{112,96},{128,112},... | collective-permute-start | bytes 49160 | tf_op jit(solution)/shard_map/ppermute | solution.py:21
  576.3 22.2 %collective-permute-start.34 = (bf16[64,128]{1,0:T(8,128)(2,1)S(1)}, bf16[64,128]{1,0:T(8,128)(2,1)S(1)}, u32[]{:S(2)}, u32[]{:S(2)}) collective-permute-start(bf16[64,128]{1,0:T(8,128)(2,1)S(1)} %bitcast.416), channel_id=1, source_target_pairs={{16,0},{32,16},{48,32},{64,48},{80,64},{96,80},{112,96},{128,112},... | collective-permute-start | bytes 49160 | tf_op jit(solution)/shard_map/ppermute | solution.py:21
  578.3 36.9 %collective-permute-start.33 = (bf16[64,128]{1,0:T(8,128)(2,1)S(1)}, bf16[64,128]{1,0:T(8,128)(2,1)S(1)}, u32[]{:S(2)}, u32[]{:S(2)}) collective-permute-start(bf16[64,128]{1,0:T(8,128)(2,1)S(1)} %bitcast.421), channel_id=1, source_target_pairs={{16,0},{32,16},{48,32},{64,48},{80,64},{96,80},{112,96},{128,112},... | collective-permute-start | bytes 49160 | tf_op jit(solution)/shard_map/ppermute | solution.py:21
  580.2 35.6 %collective-permute-start.25 = (bf16[64,128]{1,0:T(8,128)(2,1)S(1)}, bf16[64,128]{1,0:T(8,128)(2,1)S(1)}, u32[]{:S(2)}, u32[]{:S(2)}) collective-permute-start(bf16[64,128]{1,0:T(8,128)(2,1)S(1)} %collective-permute-done.24), channel_id=1, source_target_pairs={{0,1},{1,2},{2,3},{3,4},{4,5},{5,6},{6,7},{7,8},{8,9},{9,10},{10,1... | collective-permute-start | bytes 49160 | tf_op jit(solution)/shard_map/ppermute | solution.py:21
  582.1 34.3 %collective-permute-start.28 = (bf16[64,128]{1,0:T(8,128)(2,1)S(1)}, bf16[64,128]{1,0:T(8,128)(2,1)S(1)}, u32[]{:S(2)}, u32[]{:S(2)}) collective-permute-start(bf16[64,128]{1,0:T(8,128)(2,1)S(1)} %collective-permute-done.27), channel_id=1, source_target_pairs={{1,0},{2,1},{3,2},{4,3},{5,4},{6,5},{7,6},{8,7},{9,8},{10,9},{11,1... | collective-permute-start | bytes 49160 | tf_op jit(solution)/shard_map/ppermute | solution.py:21
  596.6 20.4 %collective-permute-start.32 = (bf16[64,128]{1,0:T(8,128)(2,1)S(1)}, bf16[64,128]{1,0:T(8,128)(2,1)S(1)}, u32[]{:S(2)}, u32[]{:S(2)}) collective-permute-start(bf16[64,128]{1,0:T(8,128)(2,1)S(1)} %collective-permute-done.31), channel_id=1, source_target_pairs={{0,1},{1,2},{2,3},{3,4},{4,5},{5,6},{6,7},{7,8},{8,9},{9,10},{10,1... | collective-permute-start | bytes 49160 | tf_op jit(solution)/shard_map/ppermute | solution.py:21
  598.6 19.1 %collective-permute-start.35 = (bf16[64,128]{1,0:T(8,128)(2,1)S(1)}, bf16[64,128]{1,0:T(8,128)(2,1)S(1)}, u32[]{:S(2)}, u32[]{:S(2)}) collective-permute-start(bf16[64,128]{1,0:T(8,128)(2,1)S(1)} %collective-permute-done.34), channel_id=1, source_target_pairs={{1,0},{2,1},{3,2},{4,3},{5,4},{6,5},{7,6},{8,7},{9,8},{10,9},{11,1... | collective-permute-start | bytes 49160 | tf_op jit(solution)/shard_map/ppermute | solution.py:21
  741.0 349.0 %all-gather.14.cloned.1.call-start = ((), (), s32[]{:S(2)}) async-start(), calls=%async_computation.4 | async-start | bytes 3342336 | tf_op jit(solution)/shard_map/all_gather | solution.py:12
  752.8 39.2 %collective-permute-start.36 = (bf16[64,128]{1,0:T(8,128)(2,1)S(1)}, bf16[64,128]{1,0:T(8,128)(2,1)S(1)}, u32[]{:S(2)}, u32[]{:S(2)}) collective-permute-start(bf16[64,128]{1,0:T(8,128)(2,1)S(1)} %bitcast.471), channel_id=1, source_target_pairs={{0,16},{16,32},{32,48},{48,64},{64,80},{80,96},{96,112},{112,128},... | collective-permute-start | bytes 49160 | tf_op jit(solution)/shard_map/ppermute | solution.py:21
  761.0 33.0 %collective-permute-start.38 = (bf16[64,128]{1,0:T(8,128)(2,1)S(1)}, bf16[64,128]{1,0:T(8,128)(2,1)S(1)}, u32[]{:S(2)}, u32[]{:S(2)}) collective-permute-start(bf16[64,128]{1,0:T(8,128)(2,1)S(1)} %bitcast.465), channel_id=1, source_target_pairs={{0,16},{16,32},{32,48},{48,64},{64,80},{80,96},{96,112},{112,128},... | collective-permute-start | bytes 49160 | tf_op jit(solution)/shard_map/ppermute | solution.py:21
  765.3 30.6 %collective-permute-start.39 = (bf16[64,128]{1,0:T(8,128)(2,1)S(1)}, bf16[64,128]{1,0:T(8,128)(2,1)S(1)}, u32[]{:S(2)}, u32[]{:S(2)}) collective-permute-start(bf16[64,128]{1,0:T(8,128)(2,1)S(1)} %bitcast.449), channel_id=1, source_target_pairs={{0,16},{16,32},{32,48},{48,64},{64,80},{80,96},{96,112},{112,128},... | collective-permute-start | bytes 49160 | tf_op jit(solution)/shard_map/ppermute | solution.py:21
  775.6 22.3 %collective-permute-start.41 = (bf16[64,128]{1,0:T(8,128)(2,1)S(1)}, bf16[64,128]{1,0:T(8,128)(2,1)S(1)}, u32[]{:S(2)}, u32[]{:S(2)}) collective-permute-start(bf16[64,128]{1,0:T(8,128)(2,1)S(1)} %bitcast.440), channel_id=1, source_target_pairs={{0,1},{1,2},{2,3},{3,4},{4,5},{5,6},{6,7},{7,8},{8,9},{9,10},{10,1... | collective-permute-start | bytes 49160 | tf_op jit(solution)/shard_map/ppermute | solution.py:21
  777.5 22.3 %collective-permute-start.42 = (bf16[64,128]{1,0:T(8,128)(2,1)S(1)}, bf16[64,128]{1,0:T(8,128)(2,1)S(1)}, u32[]{:S(2)}, u32[]{:S(2)}) collective-permute-start(bf16[64,128]{1,0:T(8,128)(2,1)S(1)} %bitcast.431), channel_id=1, source_target_pairs={{1,0},{2,1},{3,2},{4,3},{5,4},{6,5},{7,6},{8,7},{9,8},{10,9},{11,1... | collective-permute-start | bytes 49160 | tf_op jit(solution)/shard_map/ppermute | solution.py:21
  792.0 22.2 %collective-permute-start.43 = (bf16[64,128]{1,0:T(8,128)(2,1)S(1)}, bf16[64,128]{1,0:T(8,128)(2,1)S(1)}, u32[]{:S(2)}, u32[]{:S(2)}) collective-permute-start(bf16[64,128]{1,0:T(8,128)(2,1)S(1)} %bitcast.426), channel_id=1, source_target_pairs={{16,0},{32,16},{48,32},{64,48},{80,64},{96,80},{112,96},{128,112},... | collective-permute-start | bytes 49160 | tf_op jit(solution)/shard_map/ppermute | solution.py:21
  794.0 22.2 %collective-permute-start.46 = (bf16[64,128]{1,0:T(8,128)(2,1)S(1)}, bf16[64,128]{1,0:T(8,128)(2,1)S(1)}, u32[]{:S(2)}, u32[]{:S(2)}) collective-permute-start(bf16[64,128]{1,0:T(8,128)(2,1)S(1)} %bitcast.417), channel_id=1, source_target_pairs={{16,0},{32,16},{48,32},{64,48},{80,64},{96,80},{112,96},{128,112},... | collective-permute-start | bytes 49160 | tf_op jit(solution)/shard_map/ppermute | solution.py:21
  795.9 36.7 %collective-permute-start.45 = (bf16[64,128]{1,0:T(8,128)(2,1)S(1)}, bf16[64,128]{1,0:T(8,128)(2,1)S(1)}, u32[]{:S(2)}, u32[]{:S(2)}) collective-permute-start(bf16[64,128]{1,0:T(8,128)(2,1)S(1)} %bitcast.422), channel_id=1, source_target_pairs={{16,0},{32,16},{48,32},{64,48},{80,64},{96,80},{112,96},{128,112},... | collective-permute-start | bytes 49160 | tf_op jit(solution)/shard_map/ppermute | solution.py:21
  797.9 35.4 %collective-permute-start.37 = (bf16[64,128]{1,0:T(8,128)(2,1)S(1)}, bf16[64,128]{1,0:T(8,128)(2,1)S(1)}, u32[]{:S(2)}, u32[]{:S(2)}) collective-permute-start(bf16[64,128]{1,0:T(8,128)(2,1)S(1)} %collective-permute-done.36), channel_id=1, source_target_pairs={{0,1},{1,2},{2,3},{3,4},{4,5},{5,6},{6,7},{7,8},{8,9},{9,10},{10,1... | collective-permute-start | bytes 49160 | tf_op jit(solution)/shard_map/ppermute | solution.py:21
  799.8 34.1 %collective-permute-start.40 = (bf16[64,128]{1,0:T(8,128)(2,1)S(1)}, bf16[64,128]{1,0:T(8,128)(2,1)S(1)}, u32[]{:S(2)}, u32[]{:S(2)}) collective-permute-start(bf16[64,128]{1,0:T(8,128)(2,1)S(1)} %collective-permute-done.39), channel_id=1, source_target_pairs={{1,0},{2,1},{3,2},{4,3},{5,4},{6,5},{7,6},{8,7},{9,8},{10,9},{11,1... | collective-permute-start | bytes 49160 | tf_op jit(solution)/shard_map/ppermute | solution.py:21
  814.3 20.3 %collective-permute-start.44 = (bf16[64,128]{1,0:T(8,128)(2,1)S(1)}, bf16[64,128]{1,0:T(8,128)(2,1)S(1)}, u32[]{:S(2)}, u32[]{:S(2)}) collective-permute-start(bf16[64,128]{1,0:T(8,128)(2,1)S(1)} %collective-permute-done.43), channel_id=1, source_target_pairs={{0,1},{1,2},{2,3},{3,4},{4,5},{5,6},{6,7},{7,8},{8,9},{9,10},{10,1... | collective-permute-start | bytes 49160 | tf_op jit(solution)/shard_map/ppermute | solution.py:21
  816.2 19.0 %collective-permute-start.47 = (bf16[64,128]{1,0:T(8,128)(2,1)S(1)}, bf16[64,128]{1,0:T(8,128)(2,1)S(1)}, u32[]{:S(2)}, u32[]{:S(2)}) collective-permute-start(bf16[64,128]{1,0:T(8,128)(2,1)S(1)} %collective-permute-done.46), channel_id=1, source_target_pairs={{1,0},{2,1},{3,2},{4,3},{5,4},{6,5},{7,6},{8,7},{9,8},{10,9},{11,1... | collective-permute-start | bytes 49160 | tf_op jit(solution)/shard_map/ppermute | solution.py:21
  1099.9 26.4 %collective-permute-start.48 = (bf16[64,128]{1,0:T(8,128)(2,1)S(1)}, bf16[64,128]{1,0:T(8,128)(2,1)}, u32[]{:S(2)}, u32[]{:S(2)}) collective-permute-start(bf16[64,128]{1,0:T(8,128)(2,1)S(1)} %bitcast.472), channel_id=1, source_target_pairs={{0,16},{16,32},{32,48},{48,64},{64,80},{80,96},{96,112},{112,128},... | collective-permute-start | bytes 49160 | tf_op jit(solution)/shard_map/ppermute | solution.py:21
  1103.3 27.8 %collective-permute-start.50 = (bf16[64,128]{1,0:T(8,128)(2,1)S(1)}, bf16[64,128]{1,0:T(8,128)(2,1)S(1)}, u32[]{:S(2)}, u32[]{:S(2)}) collective-permute-start(bf16[64,128]{1,0:T(8,128)(2,1)S(1)} %bitcast.467), channel_id=1, source_target_pairs={{0,16},{16,32},{32,48},{48,64},{64,80},{80,96},{96,112},{112,128},... | collective-permute-start | bytes 49160 | tf_op jit(solution)/shard_map/ppermute | solution.py:21
  1106.7 27.5 %collective-permute-start.51 = (bf16[64,128]{1,0:T(8,128)(2,1)S(1)}, bf16[64,128]{1,0:T(8,128)(2,1)}, u32[]{:S(2)}, u32[]{:S(2)}) collective-permute-start(bf16[64,128]{1,0:T(8,128)(2,1)S(1)} %bitcast.450), channel_id=1, source_target_pairs={{0,16},{16,32},{32,48},{48,64},{64,80},{80,96},{96,112},{112,128},... | collective-permute-start | bytes 49160 | tf_op jit(solution)/shard_map/ppermute | solution.py:21
  1109.8 26.8 %collective-permute-start.53 = (bf16[64,128]{1,0:T(8,128)(2,1)S(1)}, bf16[64,128]{1,0:T(8,128)(2,1)S(1)}, u32[]{:S(2)}, u32[]{:S(2)}) collective-permute-start(bf16[64,128]{1,0:T(8,128)(2,1)S(1)} %bitcast.441), channel_id=1, source_target_pairs={{0,1},{1,2},{2,3},{3,4},{4,5},{5,6},{6,7},{7,8},{8,9},{9,10},{10,1... | collective-permute-start | bytes 49160 | tf_op jit(solution)/shard_map/ppermute | solution.py:21
  1111.8 26.9 %collective-permute-start.54 = (bf16[64,128]{1,0:T(8,128)(2,1)S(1)}, bf16[64,128]{1,0:T(8,128)(2,1)S(1)}, u32[]{:S(2)}, u32[]{:S(2)}) collective-permute-start(bf16[64,128]{1,0:T(8,128)(2,1)S(1)} %bitcast.432), channel_id=1, source_target_pairs={{1,0},{2,1},{3,2},{4,3},{5,4},{6,5},{7,6},{8,7},{9,8},{10,9},{11,1... | collective-permute-start | bytes 49160 | tf_op jit(solution)/shard_map/ppermute | solution.py:21
  1126.3 26.8 %collective-permute-start.55 = (bf16[64,128]{1,0:T(8,128)(2,1)S(1)}, bf16[64,128]{1,0:T(8,128)(2,1)}, u32[]{:S(2)}, u32[]{:S(2)}) collective-permute-start(bf16[64,128]{1,0:T(8,128)(2,1)S(1)} %bitcast.427), channel_id=1, source_target_pairs={{16,0},{32,16},{48,32},{64,48},{80,64},{96,80},{112,96},{128,112},... | collective-permute-start | bytes 49160 | tf_op jit(solution)/shard_map/ppermute | solution.py:21
  1131.1 23.9 %collective-permute-start.58 = (bf16[64,128]{1,0:T(8,128)(2,1)S(1)}, bf16[64,128]{1,0:T(8,128)(2,1)}, u32[]{:S(2)}, u32[]{:S(2)}) collective-permute-start(bf16[64,128]{1,0:T(8,128)(2,1)S(1)} %bitcast.418), channel_id=1, source_target_pairs={{16,0},{32,16},{48,32},{64,48},{80,64},{96,80},{112,96},{128,112},... | collective-permute-start | bytes 49160 | tf_op jit(solution)/shard_map/ppermute | solution.py:21
  1134.2 40.2 %collective-permute-start.57 = (bf16[64,128]{1,0:T(8,128)(2,1)}, bf16[64,128]{1,0:T(8,128)(2,1)}, u32[]{:S(2)}, u32[]{:S(2)}) collective-permute-start(bf16[64,128]{1,0:T(8,128)(2,1)} %bitcast.355), channel_id=1, source_target_pairs={{16,0},{32,16},{48,32},{64,48},{80,64},{96,80},{112,96},{128,112},... | collective-permute-start | bytes 49160 | tf_op jit(solution)/shard_map/ppermute | solution.py:21
  1136.7 39.1 %collective-permute-start.49 = (bf16[64,128]{1,0:T(8,128)(2,1)}, bf16[64,128]{1,0:T(8,128)(2,1)}, u32[]{:S(2)}, u32[]{:S(2)}) collective-permute-start(bf16[64,128]{1,0:T(8,128)(2,1)} %collective-permute-done.48), channel_id=1, source_target_pairs={{0,1},{1,2},{2,3},{3,4},{4,5},{5,6},{6,7},{7,8},{8,9},{9,10},{10,1... | collective-permute-start | bytes 49160 | tf_op jit(solution)/shard_map/ppermute | solution.py:21
  1138.6 38.5 %collective-permute-start.52 = (bf16[64,128]{1,0:T(8,128)(2,1)}, bf16[64,128]{1,0:T(8,128)(2,1)}, u32[]{:S(2)}, u32[]{:S(2)}) collective-permute-start(bf16[64,128]{1,0:T(8,128)(2,1)} %collective-permute-done.51), channel_id=1, source_target_pairs={{1,0},{2,1},{3,2},{4,3},{5,4},{6,5},{7,6},{8,7},{9,8},{10,9},{11,1... | collective-permute-start | bytes 49160 | tf_op jit(solution)/shard_map/ppermute | solution.py:21
  1153.1 25.4 %collective-permute-start.56 = (bf16[64,128]{1,0:T(8,128)(2,1)}, bf16[64,128]{1,0:T(8,128)(2,1)}, u32[]{:S(2)}, u32[]{:S(2)}) collective-permute-start(bf16[64,128]{1,0:T(8,128)(2,1)} %collective-permute-done.55), channel_id=1, source_target_pairs={{0,1},{1,2},{2,3},{3,4},{4,5},{5,6},{6,7},{7,8},{8,9},{9,10},{10,1... | collective-permute-start | bytes 49160 | tf_op jit(solution)/shard_map/ppermute | solution.py:21
  1155.0 24.8 %collective-permute-start.59 = (bf16[64,128]{1,0:T(8,128)(2,1)}, bf16[64,128]{1,0:T(8,128)(2,1)}, u32[]{:S(2)}, u32[]{:S(2)}) collective-permute-start(bf16[64,128]{1,0:T(8,128)(2,1)} %collective-permute-done.58), channel_id=1, source_target_pairs={{1,0},{2,1},{3,2},{4,3},{5,4},{6,5},{7,6},{8,7},{9,8},{10,9},{11,1... | collective-permute-start | bytes 49160 | tf_op jit(solution)/shard_map/ppermute | solution.py:21
  (24 other events, 1020.6 us)
Sparse Core Ops, SparseCore 0:
  96.2 134.4 all-gather.5
  306.0 131.6 all-gather.7
  523.5 131.7 all-gather.9
  741.1 131.7 all-gather.11
  958.6 131.3 all-gather.13
